TPU v7x, 512 devices: a whole 4x4x16 slice. The times are simulated.
512 devices in a mesh: dp: 8 (over x, core), expert: 64 (over y, z).
Axes of the slice: x: 4, y: 4, z: 16, core: 2. Of those that a mesh axis runs over, the one named last changes fastest.
Arguments:
- tokens: bfloat16 [65536, 1024], P(('dp', 'expert')), may hold values from -6 to 6
- grad_out: bfloat16 [65536, 1024], P(('dp', 'expert')), may hold values from -6 to 6
- expert_ids: int32 [65536, 8], P(('dp', 'expert')), may hold values from 0 to 63, all different within a row; in each aligned block of 128 rows (0 to 127, 128 to 255, ...) at most 18 rows name the same one
- gates: float32 [65536, 8], P(('dp', 'expert')), may hold values from 0.1 to 0.5
- w_in: bfloat16 [64, 1024, 768], P('expert', 'dp'), may hold values from -0.1875 to 0.1875
- w_down: bfloat16 [64, 384, 1024], P('expert', 'dp'), may hold values from -0.3125 to 0.3125
Outputs:
- grad_tokens: bfloat16 [65536, 1024], P(('dp', 'expert'))
- grad_in: float32 [64, 1024, 768], P('expert', 'dp')
- grad_down: float32 [64, 384, 1024], P('expert', 'dp')
Inputs may be any that keep to these rules, and one draw needn't show every extreme that they name: `expert_ids`: each token names 8 different experts; among the tokens of one device no expert is named more than 18 times, a bound that some block reaches.
All inputs are finite; a program needn't handle non-finite values.
Results may differ from a plain program's by a relative error of at most 0.015.
Values may be sent and summed in bfloat16 or wider, within the bound.
No kernel may reach another device: no remote copies, remote signals or barrier semaphores. Data moves between devices by JAX's collectives and lax.ppermute only.
A program may use at most 64 MiB of HBM per device.

v0:
```python
import jax
import jax.numpy as jnp
from jax import lax
from jax.sharding import PartitionSpec as P


def hidden_from(preact):
    half_width = preact.shape[1] // 2
    gate_pre = preact[:, :half_width]
    up_pre = preact[:, half_width:]
    sigmoid_gate = jax.nn.sigmoid(gate_pre)
    return (gate_pre * sigmoid_gate * up_pre).astype(jnp.bfloat16)


def pre_grads(preact, grad_hidden):
    half_width = preact.shape[1] // 2
    gate_pre = preact[:, :half_width]
    up_pre = preact[:, half_width:]
    sigmoid_gate = jax.nn.sigmoid(gate_pre)
    grad_gate = grad_hidden * up_pre * sigmoid_gate * (1.0 + gate_pre * (1.0 - sigmoid_gate))
    grad_up = grad_hidden * gate_pre * sigmoid_gate
    return jnp.concatenate([grad_gate, grad_up], axis=1).astype(jnp.bfloat16)


def contract_first(left, right):
    return lax.dot_general(
        left, right, (((0,), (0,)), ((), ())), preferred_element_type=jnp.float32
    )


def contract_last(left, right):
    return lax.dot_general(
        left, right, (((1,), (1,)), ((), ())), preferred_element_type=jnp.float32
    )


def on_device(tokens, grad_out, expert_ids, gates, w_in, w_down):
    token_rows, model_width = tokens.shape
    route_width = expert_ids.shape[1]
    expert_count = lax.axis_size("expert")
    route_total = token_rows * route_width
    capacity = route_total // expert_count + max(1, route_total // (8 * expert_count))
    slot_total = expert_count * capacity
    flat_ids = expert_ids.reshape(route_total)
    route_marks = (flat_ids[:, None] == jnp.arange(expert_count, dtype=jnp.int32)[None, :]).astype(
        jnp.int32
    )
    route_index = jnp.arange(route_total, dtype=jnp.int32)
    lower_table = (route_index[None, :] <= route_index[:, None]).astype(jnp.bfloat16)
    running = jnp.dot(
        lower_table, route_marks.astype(jnp.bfloat16), preferred_element_type=jnp.float32
    )
    slot_ranks = jnp.sum((running.astype(jnp.int32) - 1) * route_marks, axis=1)
    targets = flat_ids * capacity + slot_ranks
    route_of_slot = jnp.full((slot_total,), route_total, jnp.int32).at[targets].set(route_index)
    occupied = route_of_slot < route_total
    clipped = jnp.minimum(route_of_slot, route_total - 1)
    source_rows = clipped // route_width
    slot_gates = jnp.where(
        occupied, gates.reshape(route_total)[clipped], jnp.zeros((), jnp.float32)
    )
    send_tokens = jnp.where(occupied[:, None], tokens[source_rows], jnp.zeros((), jnp.bfloat16))
    send_grads = (slot_gates[:, None] * grad_out[source_rows].astype(jnp.float32)).astype(
        jnp.bfloat16
    )
    recv_tokens, recv_grads = (
        lax.all_to_all(
            send_tokens.reshape(expert_count, capacity, model_width),
            "expert",
            split_axis=0,
            concat_axis=0,
            tiled=True,
        ),
        lax.all_to_all(
            send_grads.reshape(expert_count, capacity, model_width),
            "expert",
            split_axis=0,
            concat_axis=0,
            tiled=True,
        ),
    )
    slot_tokens = recv_tokens.reshape(slot_total, model_width)
    slot_grads = recv_grads.reshape(slot_total, model_width)
    local_in = w_in[0]
    local_down = w_down[0]
    full_in, full_down = (
        lax.all_gather(local_in, "dp", axis=0, tiled=True),
        lax.all_gather(local_down, "dp", axis=0, tiled=True),
    )
    preact = jnp.dot(slot_tokens, full_in, preferred_element_type=jnp.float32)
    grad_hidden = contract_last(slot_grads, full_down)
    pre_grad = pre_grads(preact, grad_hidden)
    slot_back = contract_last(pre_grad, full_in).astype(jnp.bfloat16)
    hidden_act = hidden_from(preact)
    columns = slot_tokens
    grad_in_local = lax.psum_scatter(
        contract_first(columns, pre_grad).astype(jnp.bfloat16),
        "dp",
        scatter_dimension=0,
        tiled=True,
    ).astype(jnp.float32)
    columns = hidden_act
    grad_down_local = lax.psum_scatter(
        contract_first(columns, slot_grads).astype(jnp.bfloat16),
        "dp",
        scatter_dimension=0,
        tiled=True,
    ).astype(jnp.float32)
    slot_return = lax.all_to_all(
        slot_back.reshape(expert_count, capacity, model_width),
        "expert",
        split_axis=0,
        concat_axis=0,
        tiled=True,
    )
    per_route = slot_return.reshape(slot_total, model_width)[targets]
    grad_tokens = jnp.sum(
        per_route.reshape(token_rows, route_width, model_width).astype(jnp.float32), axis=1
    ).astype(jnp.bfloat16)
    return (grad_tokens, grad_in_local[None], grad_down_local[None])


def solution(mesh):
    in_specs = (
        P(("dp", "expert"), None),
        P(("dp", "expert"), None),
        P(("dp", "expert"), None),
        P(("dp", "expert"), None),
        P("expert", "dp", None),
        P("expert", "dp", None),
    )
    out_specs = (P(("dp", "expert"), None), P("expert", "dp", None), P("expert", "dp", None))
    return jax.shard_map(
        on_device, mesh=mesh, in_specs=in_specs, out_specs=out_specs, check_vma=False
    )
```

profile of v0, /device:TPU:6, one launch (start us, length us, event | category | flops | bytes accessed | tf_op | source)
XLA Modules:
  0.0 525.3 jit_solution(16748239414369086779)
XLA Ops:
  7.2 0.8 copy.10
  9.6 4.3 scatter_custom_fusion
  14.9 4.6 gather_fusion
  19.6 5.0 gather_fusion.2
  24.6 2.7 gather.17
  27.3 1.8 broadcast_select_fusion
  29.2 19.1 %all-to-all-start.1 = ((bf16[64,18,1024]{2,1,0:T(8,128)(2,1)}), bf16[64,18,1024]{2,1,0:T(8,128)(2,1)}, u32[]{:S(2)}, u32[]{:S(2)}) async-start(bf16[64,18,1024]{2,1,0:T(8,128)(2,1)} %broadcast_select_fusion), calls=%async_computation.1 | async-start | bytes 6291456 | tf_op jit(solution)/shard_map/all_to_all | solution.py:67
  48.4 4.4 gather_fusion.1
  52.8 3.2 reshape.78
  56.0 4.8 multiply_convert_fusion
  60.8 130.9 %all-to-all-done.1 = bf16[64,18,1024]{2,1,0:T(8,128)(2,1)} async-done(((bf16[64,18,1024]{2,1,0:T(8,128)(2,1)}), bf16[64,18,1024]{2,1,0:T(8,128)(2,1)}, u32[]{:S(2)}, u32[]{:S(2)}) %all-to-all-start.1) | async-done | bytes 2359328 | tf_op jit(solution)/shard_map/all_to_all | solution.py:67
  191.8 7.0 %all-to-all-start = ((bf16[64,18,1024]{2,1,0:T(8,128)(2,1)}), bf16[64,18,1024]{2,1,0:T(8,128)(2,1)S(1)}, u32[]{:S(2)}, u32[]{:S(2)}) async-start(bf16[64,18,1024]{2,1,0:T(8,128)(2,1)} %multiply_convert_fusion), calls=%async_computation | async-start | bytes 6291456 | tf_op jit(solution)/shard_map/all_to_all | solution.py:74
  199.5 14.6 %all-gather = bf16[1,384,1024]{2,1,0:T(8,128)(2,1)} all-gather(bf16[1,48,1024]{2,1,0:T(8,128)(2,1)S(1)} %copy-done.5), channel_id=2, replica_groups=mesh['dp'=8,'expert'=64] {'dp'}, dimensions={1}, use_global_device_ids=true | all-gather | bytes 884736 | tf_op jit(solution)/shard_map/all_gather | solution.py:88
  214.1 4.4 reshape.74
  218.5 123.5 %all-to-all-done = bf16[64,18,1024]{2,1,0:T(8,128)(2,1)S(1)} async-done(((bf16[64,18,1024]{2,1,0:T(8,128)(2,1)}), bf16[64,18,1024]{2,1,0:T(8,128)(2,1)S(1)}, u32[]{:S(2)}, u32[]{:S(2)}) %all-to-all-start) | async-done | bytes 2359328 | tf_op jit(solution)/shard_map/all_to_all | solution.py:74
  342.0 2.2 reshape.73
  344.2 4.5 fusion.2
  348.8 1.5 multiply_convert_fusion.3
  350.5 0.9 copy-done.8
  351.7 2.1 convolution_convert_fusion
  353.8 2.4 reshape.75
  356.3 7.3 %all-to-all-start.2 = ((bf16[64,18,1024]{2,1,0:T(8,128)(2,1)}), bf16[64,18,1024]{2,1,0:T(8,128)(2,1)}, u32[]{:S(2)}, u32[]{:S(2)}) async-start(bf16[64,18,1024]{2,1,0:T(8,128)(2,1)} %reshape.75), calls=%async_computation.2 | async-start | bytes 6291456 | tf_op jit(solution)/shard_map/all_to_all | solution.py:109
  363.6 5.0 convolution_convert_fusion.2
  368.9 4.6 convolution_convert_fusion.1
  373.5 33.3 %reduce-scatter.5.cloned.1.call-done = bf16[48,1024]{1,0:T(8,128)(2,1)} async-done(((bf16[384,1024]{1,0:T(8,128)(2,1)}), bf16[48,1024]{1,0:T(8,128)(2,1)}) %reduce-scatter.5.cloned.1.call-update) | async-done | bytes 98320 | tf_op jit(solution)/shard_map/reduce_scatter | solution.py:103
  406.8 1.6 bitcast_convert_fusion.1
  408.4 41.9 %reduce-scatter.3.cloned.1.call-done = bf16[128,768]{1,0:T(8,128)(2,1)} async-done(((bf16[1024,768]{1,0:T(8,128)(2,1)}), bf16[128,768]{1,0:T(8,128)(2,1)}) %reduce-scatter.3.cloned.1.call-update) | async-done | bytes 196624 | tf_op jit(solution)/shard_map/reduce_scatter | solution.py:96
  450.3 1.7 bitcast_convert_fusion
  451.9 54.8 %all-to-all-done.2 = bf16[64,18,1024]{2,1,0:T(8,128)(2,1)} async-done(((bf16[64,18,1024]{2,1,0:T(8,128)(2,1)}), bf16[64,18,1024]{2,1,0:T(8,128)(2,1)}, u32[]{:S(2)}, u32[]{:S(2)}) %all-to-all-start.2) | async-done | bytes 2359328 | tf_op jit(solution)/shard_map/all_to_all | solution.py:109
  506.7 2.9 reshape.76
  509.7 5.4 %gather_fusion.3 = bf16[1024,1024]{1,0:T(8,128)(2,1)} fusion(bf16[1152,1024]{1,0:T(8,128)(2,1)S(1)} %reshape.76, s32[1024]{0:T(1024)S(1)} %broadcast_clamp_fusion), kind=kCustom, calls=%fused_computation.3 | custom fusion | bytes 4198400 | tf_op jit(solution)/shard_map/gather | solution.py:116
  515.1 3.7 bitcast_reduce_fusion
  (43 shorter events, 4.4 us)
Async XLA Ops:
  7.2 12.4 %copy-start = (bf16[128,1024]{1,0:T(8,128)(2,1)S(1)}, bf16[128,1024]{1,0:T(8,128)(2,1)}, u32[]{:S(2)}) copy-start(bf16[128,1024]{1,0:T(8,128)(2,1)} %param.6) | copy-start | bytes 786436
  29.2 19.2 %copy-start.1 = (bf16[128,1024]{1,0:T(8,128)(2,1)S(1)}, bf16[128,1024]{1,0:T(8,128)(2,1)}, u32[]{:S(2)}) copy-start(bf16[128,1024]{1,0:T(8,128)(2,1)} %param.7) | copy-start | bytes 786436
  29.2 162.6 %all-to-all-start.1 = ((bf16[64,18,1024]{2,1,0:T(8,128)(2,1)}), bf16[64,18,1024]{2,1,0:T(8,128)(2,1)}, u32[]{:S(2)}, u32[]{:S(2)}) async-start(bf16[64,18,1024]{2,1,0:T(8,128)(2,1)} %broadcast_select_fusion), calls=%async_computation.1 | async-start | bytes 6291456 | tf_op jit(solution)/shard_map/all_to_all | solution.py:67
  60.8 138.6 %copy-start.5 = (bf16[1,48,1024]{2,1,0:T(8,128)(2,1)S(1)}, bf16[1,48,1024]{2,1,0:T(8,128)(2,1)}, u32[]{:S(2)}) copy-start(bf16[1,48,1024]{2,1,0:T(8,128)(2,1)} %param.11) | copy-start | bytes 294916
  191.8 150.2 %all-to-all-start = ((bf16[64,18,1024]{2,1,0:T(8,128)(2,1)}), bf16[64,18,1024]{2,1,0:T(8,128)(2,1)S(1)}, u32[]{:S(2)}, u32[]{:S(2)}) async-start(bf16[64,18,1024]{2,1,0:T(8,128)(2,1)} %multiply_convert_fusion), calls=%async_computation | async-start | bytes 6291456 | tf_op jit(solution)/shard_map/all_to_all | solution.py:74
  198.7 145.5 %all-gather.4.cloned.1.call-start = ((), (), s32[]{:S(2)}) async-start(), calls=%async_computation.7 | async-start | bytes 1769472 | tf_op jit(solution)/shard_map/all_gather | solution.py:87
  344.2 4.5 copy-start.3
  344.2 4.5 copy-start.4
  348.8 1.8 copy-start.7
  348.8 3.0 copy-start.6
  350.5 0.9 copy-start.8
  350.5 1.2 copy-start.10
  356.3 150.5 %all-to-all-start.2 = ((bf16[64,18,1024]{2,1,0:T(8,128)(2,1)}), bf16[64,18,1024]{2,1,0:T(8,128)(2,1)}, u32[]{:S(2)}, u32[]{:S(2)}) async-start(bf16[64,18,1024]{2,1,0:T(8,128)(2,1)} %reshape.75), calls=%async_computation.2 | async-start | bytes 6291456 | tf_op jit(solution)/shard_map/all_to_all | solution.py:109
  363.5 5.3 %copy-start.2 = (bf16[1152,1024]{1,0:T(8,128)(2,1)S(1)}, bf16[1152,1024]{1,0:T(8,128)(2,1)}, u32[]{:S(2)}) copy-start(bf16[1152,1024]{1,0:T(8,128)(2,1)} %reshape.74) | copy-start | bytes 7077892
  363.5 5.3 %copy-start.9 = (bf16[1152,384]{0,1:T(8,128)(2,1)S(1)}, bf16[1152,384]{0,1:T(8,128)(2,1)}, u32[]{:S(2)}) copy-start(bf16[1152,384]{0,1:T(8,128)(2,1)} %copy-done.8) | copy-start | bytes 2654212
  363.5 43.2 %reduce-scatter.5.cloned.1.call-start = ((), (), s32[]{:S(2)}) async-start(), calls=%async_computation.6 | async-start | bytes 884736 | tf_op jit(solution)/shard_map/reduce_scatter | solution.py:103
  368.6 81.6 %reduce-scatter.3.cloned.1.call-start = ((), (), s32[]{:S(2)}) async-start(), calls=%async_computation.5 | async-start | bytes 1769472 | tf_op jit(solution)/shard_map/reduce_scatter | solution.py:96
Sparse Core Ops, SparseCore 0:
  201.7 31.1 all-gather.3
  368.7 38.0 reduce-scatter.4
  409.6 40.5 reduce-scatter.2
where the time goes:
time: 526 us; the launch traced here: 525 us
  waiting for transfers between devices  385 us (73%)
  local copies, waits for them, and re-layouts  45.3 us (9%)
  starting transfers between devices  33.7 us (6%)
  matrix products  18.3 us (3%)
  blocking collectives  14.6 us (3%)
  other arithmetic  14.4 us (3%)
  between operations  14 us (3%)
    all_to_all x1, waiting for transfers between devices, on_device(): lax.all_to_all(send_tokens.reshape(expert_count, capacity, model_width),...  131 us
    all_to_all x1, waiting for transfers between devices, on_device(): lax.all_to_all(send_grads.reshape(expert_count, capacity, model_width), '...  123 us
    all_to_all x1, waiting for transfers between devices, on_device(): lax.all_to_all(slot_back.reshape(expert_count, capacity, model_width), 'e...  54.8 us
    reduce_scatter x1, waiting for transfers between devices, on_device(): lax.psum_scatter(contract_first(columns, pre_grad).astype(jnp.bfloat16),...  41.9 us
    reduce_scatter x1, waiting for transfers between devices, on_device(): lax.psum_scatter(contract_first(columns, slot_grads).astype(jnp.bfloat16)...  33.3 us
    all_to_all x1, starting transfers between devices, on_device(): lax.all_to_all(send_tokens.reshape(expert_count, capacity, model_width),...  19.1 us
    all_gather x1, blocking collectives, on_device(): lax.all_gather(local_down, 'dp', axis=0, tiled=True)  14.6 us
  transfers between devices with their start and end apart: 6, of which 5 were waited for; matrix products, arithmetic and copies ran while one was open for 6% of the time, Pallas kernels for 0%

commit v1 on v0

v1 whole, which is shorter than its diff:
```python
import jax
import jax.numpy as jnp
from jax import lax
from jax.sharding import Mesh
from jax.sharding import PartitionSpec as P


def hidden_from(preact):
    half_width = preact.shape[1] // 2
    gate_pre = preact[:, :half_width]
    up_pre = preact[:, half_width:]
    sigmoid_gate = jax.nn.sigmoid(gate_pre)
    return (gate_pre * sigmoid_gate * up_pre).astype(jnp.bfloat16)


def pre_grads(preact, grad_hidden):
    half_width = preact.shape[1] // 2
    gate_pre = preact[:, :half_width]
    up_pre = preact[:, half_width:]
    sigmoid_gate = jax.nn.sigmoid(gate_pre)
    grad_gate = grad_hidden * up_pre * sigmoid_gate * (1.0 + gate_pre * (1.0 - sigmoid_gate))
    grad_up = grad_hidden * gate_pre * sigmoid_gate
    return jnp.concatenate([grad_gate, grad_up], axis=1).astype(jnp.bfloat16)


def contract_first(left, right):
    return lax.dot_general(
        left, right, (((0,), (0,)), ((), ())), preferred_element_type=jnp.float32
    )


def contract_last(left, right):
    return lax.dot_general(
        left, right, (((1,), (1,)), ((), ())), preferred_element_type=jnp.float32
    )


def expert_exchange(blocks, rows, cols):
    capacity, width = blocks.shape[1], blocks.shape[2]
    blocks = blocks.reshape(rows, cols, capacity, width)
    blocks = lax.all_to_all(blocks, "ez", 1, 1, tiled=True)
    blocks = lax.all_to_all(blocks, "ey", 0, 0, tiled=True)
    return blocks.reshape(rows * cols, capacity, width)


def on_device(tokens, grad_out, expert_ids, gates, w_in, w_down):
    token_rows, model_width = tokens.shape
    route_width = expert_ids.shape[1]
    rows = lax.axis_size("ey")
    cols = lax.axis_size("ez")
    expert_count = rows * cols
    route_total = token_rows * route_width
    capacity = route_total // expert_count + max(1, route_total // (8 * expert_count))
    slot_total = expert_count * capacity
    flat_ids = expert_ids.reshape(route_total)
    route_marks = (flat_ids[:, None] == jnp.arange(expert_count, dtype=jnp.int32)[None, :]).astype(
        jnp.int32
    )
    route_index = jnp.arange(route_total, dtype=jnp.int32)
    lower_table = (route_index[None, :] <= route_index[:, None]).astype(jnp.bfloat16)
    running = jnp.dot(
        lower_table, route_marks.astype(jnp.bfloat16), preferred_element_type=jnp.float32
    )
    slot_ranks = jnp.sum((running.astype(jnp.int32) - 1) * route_marks, axis=1)
    targets = (flat_ids * capacity + slot_ranks).reshape(token_rows, route_width)
    slot_index = jnp.arange(slot_total, dtype=jnp.int32)
    slot_hits = targets[None, :, :] == slot_index[:, None, None]
    slot_of_token = jnp.any(slot_hits, axis=2).astype(jnp.bfloat16)
    slot_gates = jnp.sum(jnp.where(slot_hits, gates[None, :, :], 0.0), axis=(1, 2))
    send_tokens = jnp.dot(slot_of_token, tokens, preferred_element_type=jnp.float32).astype(
        jnp.bfloat16
    )
    picked_grads = jnp.dot(slot_of_token, grad_out, preferred_element_type=jnp.float32)
    send_grads = (slot_gates[:, None] * picked_grads).astype(jnp.bfloat16)
    send_both = jnp.concatenate([send_tokens, send_grads], axis=1)
    recv_both = expert_exchange(
        send_both.reshape(expert_count, capacity, 2 * model_width), rows, cols
    ).reshape(slot_total, 2 * model_width)
    slot_tokens = recv_both[:, :model_width]
    slot_grads = recv_both[:, model_width:]
    local_in = w_in[0]
    local_down = w_down[0]
    full_in, full_down = (
        lax.all_gather(local_in, "dp", axis=0, tiled=True),
        lax.all_gather(local_down, "dp", axis=0, tiled=True),
    )
    preact = jnp.dot(slot_tokens, full_in, preferred_element_type=jnp.float32)
    grad_hidden = contract_last(slot_grads, full_down)
    pre_grad = pre_grads(preact, grad_hidden)
    slot_back = contract_last(pre_grad, full_in).astype(jnp.bfloat16)
    hidden_act = hidden_from(preact)
    grad_in_local = lax.psum_scatter(
        contract_first(slot_tokens, pre_grad).astype(jnp.bfloat16),
        "dp",
        scatter_dimension=0,
        tiled=True,
    ).astype(jnp.float32)
    grad_down_local = lax.psum_scatter(
        contract_first(hidden_act, slot_grads).astype(jnp.bfloat16),
        "dp",
        scatter_dimension=0,
        tiled=True,
    ).astype(jnp.float32)
    slot_return = expert_exchange(
        slot_back.reshape(expert_count, capacity, model_width), rows, cols
    ).reshape(slot_total, model_width)
    grad_tokens = contract_first(slot_of_token, slot_return).astype(jnp.bfloat16)
    return (grad_tokens, grad_in_local[None], grad_down_local[None])


def solution(mesh):
    dp_size = mesh.shape["dp"]
    expert_devices = mesh.devices.reshape(dp_size, -1)
    rows = 4 if expert_devices.shape[1] % 4 == 0 else 1
    split_mesh = Mesh(
        expert_devices.reshape(dp_size, rows, expert_devices.shape[1] // rows),
        ("dp", "ey", "ez"),
    )
    token_spec = P(("dp", "ey", "ez"), None)
    weight_spec = P(("ey", "ez"), "dp", None)
    in_specs = (token_spec, token_spec, token_spec, token_spec, weight_spec, weight_spec)
    out_specs = (token_spec, weight_spec, weight_spec)
    return jax.shard_map(
        on_device, mesh=split_mesh, in_specs=in_specs, out_specs=out_specs, check_vma=False
    )
```

time: 526 us -> 532 us (1.011)
  waiting for transfers between devices: 385 us -> 152 us
  blocking collectives: 14.6 us -> 237 us
  local copies, waits for them, and re-layouts: 45.3 us -> 58.2 us
  starting transfers between devices: 33.7 us -> 22.6 us
  matrix products: 18.3 us -> 25.5 us
  other arithmetic: 14.4 us -> 20.1 us
    all_to_all x0 -> x1, blocking collectives: none -> 224 us  [expert_exchange(): blocks = lax.all_to_all(blocks, 'ez', 1, 1, tiled=True)]
    all_to_all x3, waiting for transfers between devices: 309 us -> 152 us  [the longest x1 95.3 us: expert_exchange(): blocks = lax.all_to_all(blocks, 'ez', 1, 1, tiled=True)]
    reduce_scatter x2, waiting for transfers between devices: 75.1 us -> 0.02 us  [the longest x1 0.02 us: on_device(): lax.psum_scatter(contract_first(hidden_act, slot_grads).astype(jnp.bfloat...]
    another operation x0 -> x6, local copies, waits for them, and re-layouts: none -> 30.5 us  [the longest x4 20.5 us: expert_exchange(): blocks = blocks.reshape(rows, cols, capacity, width)]
    gather x5 -> x0, local copies, waits for them, and re-layouts: 22.1 us -> none  [the longest x2 7.73 us: on_device(): tokens[source_rows]]
    all_to_all x0 -> x4, local copies, waits for them, and re-layouts: none -> 18.4 us  [the longest x2 11 us: expert_exchange(): blocks = lax.all_to_all(blocks, 'ey', 0, 0, tiled=True)]
    reshape x5 -> x0, local copies, waits for them, and re-layouts: 12.1 us -> none  [the longest x1 4.39 us: on_device(): slot_tokens = recv_tokens.reshape(slot_total, model_width)]
    all_to_all x3, starting transfers between devices: 33.3 us -> 22.2 us  [the longest x1 12.7 us: expert_exchange(): blocks = lax.all_to_all(blocks, 'ez', 1, 1, tiled=True)]
  transfers between devices with their start and end apart: 6 -> 6, of which waited for: 5 -> 3; matrix products, arithmetic and copies ran while one was open for 6% -> 6% of each run, Pallas kernels for 0% -> 0%
where the time goes in v1:
time: 532 us; the launch traced here: 530 us
  blocking collectives  237 us (45%)
  waiting for transfers between devices  152 us (29%)
  local copies, waits for them, and re-layouts  58.2 us (11%)
  matrix products  25.5 us (5%)
  starting transfers between devices  22.6 us (4%)
  other arithmetic  20.1 us (4%)
  between operations  13.9 us (3%)
    all_to_all x1, blocking collectives, expert_exchange(): blocks = lax.all_to_all(blocks, 'ez', 1, 1, tiled=True)  224 us
    all_to_all x1, waiting for transfers between devices, expert_exchange(): blocks = lax.all_to_all(blocks, 'ez', 1, 1, tiled=True)  95.3 us
    all_to_all x2, waiting for transfers between devices, expert_exchange(): blocks = lax.all_to_all(blocks, 'ey', 0, 0, tiled=True)  56.3 us
    another operation x4, local copies, waits for them, and re-layouts, expert_exchange(): blocks = blocks.reshape(rows, cols, capacity, width)  20.5 us
    dot_general x3, matrix products, contract_first(): lax.dot_general(left, right, (((0,), (0,)), ((), ())), preferred_element_...  13.4 us
    all_gather x1, blocking collectives, on_device(): lax.all_gather(local_down, 'dp', axis=0, tiled=True)  13.4 us
    all_to_all x1, starting transfers between devices, expert_exchange(): blocks = lax.all_to_all(blocks, 'ez', 1, 1, tiled=True)  12.7 us
    all_to_all x2, local copies, waits for them, and re-layouts, expert_exchange(): blocks = lax.all_to_all(blocks, 'ey', 0, 0, tiled=True)  11 us
  transfers between devices with their start and end apart: 6, of which 3 were waited for; matrix products, arithmetic and copies ran while one was open for 6% of the time, Pallas kernels for 0%

profile of v1, /device:TPU:6, one launch (start us, length us, event | category | flops | bytes accessed | tf_op | source)
XLA Modules:
  0.0 529.9 jit_solution(8605643046941876970)
XLA Ops:
  7.2 0.8 copy.38
  9.6 4.2 fusion
  13.8 9.3 %select_reduce_fusion = f32[1152]{0:T(1024)S(1)} fusion(f32[128,8]{0,1:T(8,128)} %param.9, s32[128,8]{0,1:T(8,128)S(1)} %multiply_add_fusion), kind=kLoop, calls=%fused_computation.2 | loop fusion | flops 3537792 | bytes 12800 | tf_op jit(solution)/shard_map/reduce_sum | solution.py:69
  24.8 2.5 pad_maximum_fusion
  27.3 6.8 %copy.40 = bf16[1152,2048]{1,0:T(8,128)(2,1)} copy(bf16[1152,2048]{0,1:T(8,128)(2,1)} %pad_maximum_fusion) | data formatting | bytes 9437184 | tf_op jit(solution)/shard_map/concatenate | solution.py:75
  34.1 7.6 %reshape_reshape.12 = bf16[4,16,18,2048]{3,2,1,0:T(8,128)(2,1)} reshape(bf16[1152,2048]{1,0:T(8,128)(2,1)} %copy.40) | data formatting | bytes 9437184 | tf_op jit(solution)/shard_map/reshape;reshape | solution.py:40
  41.7 6.8 %copy.41 = bf16[4,16,18,2048]{3,0,2,1:T(4,128)(2,1)S(1)} copy(bf16[4,16,18,2048]{3,2,1,0:T(8,128)(2,1)} %reshape_reshape.12) | data formatting | bytes 9437184 | tf_op jit(solution)/shard_map/reshape;reshape | solution.py:40
  48.5 223.9 %all_to_all.20 = bf16[4,16,18,2048]{3,0,2,1:T(4,128)(2,1)S(1)} all-to-all(bf16[4,16,18,2048]{3,0,2,1:T(4,128)(2,1)S(1)} %copy.41), channel_id=1, replica_groups=mesh['dp'=8,'ey'=4,'ez'=16] {'ez'}, dimensions={1} | all-to-all | bytes 9437184 | tf_op jit(solution)/shard_map/all_to_all | solution.py:41
  272.4 4.7 copy.42
  277.1 5.1 all-to-all-start.1
  282.9 13.4 %all-gather = bf16[1,384,1024]{2,1,0:T(8,128)(2,1)S(1)} all-gather(bf16[1,48,1024]{2,1,0:T(8,128)(2,1)S(1)} %copy-done.4), channel_id=2, replica_groups=mesh['dp'=8,'ey'=4,'ez'=16] {'dp'}, dimensions={1}, use_global_device_ids=true | all-gather | bytes 884736 | tf_op jit(solution)/shard_map/all_gather | solution.py:85
  296.3 34.3 %all-to-all-done.1 = bf16[4,16,18,2048]{3,1,2,0:T(8,128)(2,1)} async-done(((bf16[4,16,18,2048]{3,1,2,0:T(8,128)(2,1)}), bf16[4,16,18,2048]{3,1,2,0:T(8,128)(2,1)}, u32[]{:S(2)}, u32[]{:S(2)}) %all-to-all-start.1) | async-done | bytes 4718624 | tf_op jit(solution)/shard_map/all_to_all | solution.py:42
  330.6 7.9 %copy.43 = bf16[4,16,18,2048]{3,2,1,0:T(8,128)(2,1)} copy(bf16[4,16,18,2048]{3,1,2,0:T(8,128)(2,1)} %all-to-all-done.1) | data formatting | bytes 9437184 | tf_op jit(solution)/shard_map/all_to_all | solution.py:42
  338.5 7.7 %reshape_reshape.13 = bf16[1152,2048]{1,0:T(8,128)(2,1)} reshape(bf16[4,16,18,2048]{3,2,1,0:T(8,128)(2,1)} %copy.43) | data formatting | bytes 9437184 | tf_op jit(solution)/shard_map/reshape;reshape | solution.py:78
  346.3 4.6 fusion.5
  350.9 1.6 multiply_convert_fusion.2
  352.8 0.9 copy-done.7
  354.0 3.5 convolution_convert_fusion
  357.6 2.7 reshape_reshape.14
  360.3 3.4 copy.44
  363.7 12.7 %all-to-all-start.2 = ((bf16[4,16,18,1024]{3,0,2,1:T(4,128)(2,1)}), bf16[4,16,18,1024]{3,0,2,1:T(4,128)(2,1)S(1)}, u32[]{:S(2)}, u32[]{:S(2)}) async-start(bf16[4,16,18,1024]{3,0,2,1:T(4,128)(2,1)} %copy.44), calls=%async_computation.2 | async-start | bytes 4718592 | tf_op jit(solution)/shard_map/all_to_all | solution.py:41
  376.4 4.9 fusion.16
  381.6 5.6 %fusion.11 = bf16[1024,768]{1,0:T(8,128)(2,1)} fusion(bf16[1152,2048]{1,0:T(8,128)(2,1)} %reshape_reshape.13, bf16[1152,384]{0,1:T(8,128)(2,1)} %copy-done.8, bf16[1152,384]{0,1:T(8,128)(2,1)} %copy-done.7), kind=kOutput, calls=%fused_computation.23 | convolution fusion | flops 1816264704 | bytes 5701632 | tf_op jit(solution)/shard_map/dot_general | solution.py:27
  387.2 95.3 %all-to-all-done.2 = bf16[4,16,18,1024]{3,0,2,1:T(4,128)(2,1)S(1)} async-done(((bf16[4,16,18,1024]{3,0,2,1:T(4,128)(2,1)}), bf16[4,16,18,1024]{3,0,2,1:T(4,128)(2,1)S(1)}, u32[]{:S(2)}, u32[]{:S(2)}) %all-to-all-start.2) | async-done | bytes 2359328 | tf_op jit(solution)/shard_map/all_to_all | solution.py:41
  482.5 2.7 copy.45
  485.2 4.5 all-to-all-start.3
  489.8 1.6 bitcast_convert_fusion.1
  491.4 1.7 bitcast_convert_fusion
  493.1 22.0 %all-to-all-done.3 = bf16[4,16,18,1024]{3,1,2,0:T(8,128)(2,1)} async-done(((bf16[4,16,18,1024]{3,1,2,0:T(8,128)(2,1)}), bf16[4,16,18,1024]{3,1,2,0:T(8,128)(2,1)}, u32[]{:S(2)}, u32[]{:S(2)}) %all-to-all-start.3) | async-done | bytes 2359328 | tf_op jit(solution)/shard_map/all_to_all | solution.py:42
  515.1 3.1 copy.46
  518.2 2.2 reshape_reshape.15
  520.4 2.9 convolution_convert_fusion.2
  (33 shorter events, 4.9 us)
Async XLA Ops:
  7.2 15.9 %copy-start = (bf16[128,1024]{1,0:T(8,128)(2,1)S(1)}, bf16[128,1024]{1,0:T(8,128)(2,1)}, u32[]{:S(2)}) copy-start(bf16[128,1024]{1,0:T(8,128)(2,1)} %param.6) | copy-start | bytes 786436
  8.1 15.8 %copy-start.3 = (bf16[128,1024]{1,0:T(8,128)(2,1)S(1)}, bf16[128,1024]{1,0:T(8,128)(2,1)}, u32[]{:S(2)}) copy-start(bf16[128,1024]{1,0:T(8,128)(2,1)} %param.7) | copy-start | bytes 786436
  277.1 5.8 %copy-start.4 = (bf16[1,48,1024]{2,1,0:T(8,128)(2,1)S(1)}, bf16[1,48,1024]{2,1,0:T(8,128)(2,1)}, u32[]{:S(2)}) copy-start(bf16[1,48,1024]{2,1,0:T(8,128)(2,1)} %param.11) | copy-start | bytes 294916
  277.1 53.5 %all-to-all-start.1 = ((bf16[4,16,18,2048]{3,1,2,0:T(8,128)(2,1)}), bf16[4,16,18,2048]{3,1,2,0:T(8,128)(2,1)}, u32[]{:S(2)}, u32[]{:S(2)}) async-start(bf16[4,16,18,2048]{3,1,2,0:T(8,128)(2,1)} %copy.42), calls=%async_computation.1 | async-start | bytes 9437184 | tf_op jit(solution)/shard_map/all_to_all | solution.py:42
  282.2 64.1 %all-gather.4.cloned.1.call-start = ((), (), s32[]{:S(2)}) async-start(), calls=%async_computation.8 | async-start | bytes 1769472 | tf_op jit(solution)/shard_map/all_gather | solution.py:84
  346.3 4.7 copy-start.2
  350.9 1.9 copy-start.6
  350.9 3.1 copy-start.5
  352.8 0.9 copy-start.7
  352.8 1.2 copy-start.8
  363.7 118.8 %all-to-all-start.2 = ((bf16[4,16,18,1024]{3,0,2,1:T(4,128)(2,1)}), bf16[4,16,18,1024]{3,0,2,1:T(4,128)(2,1)S(1)}, u32[]{:S(2)}, u32[]{:S(2)}) async-start(bf16[4,16,18,1024]{3,0,2,1:T(4,128)(2,1)} %copy.44), calls=%async_computation.2 | async-start | bytes 4718592 | tf_op jit(solution)/shard_map/all_to_all | solution.py:41
  376.3 113.4 %reduce-scatter.5.cloned.1.call-start = ((), (), s32[]{:S(2)}) async-start(), calls=%async_computation.7 | async-start | bytes 884736 | tf_op jit(solution)/shard_map/reduce_scatter | solution.py:98
  381.3 110.1 %reduce-scatter.3.cloned.1.call-start = ((), (), s32[]{:S(2)}) async-start(), calls=%async_computation.6 | async-start | bytes 1769472 | tf_op jit(solution)/shard_map/reduce_scatter | solution.py:92
  485.2 29.8 %all-to-all-start.3 = ((bf16[4,16,18,1024]{3,1,2,0:T(8,128)(2,1)}), bf16[4,16,18,1024]{3,1,2,0:T(8,128)(2,1)}, u32[]{:S(2)}, u32[]{:S(2)}) async-start(bf16[4,16,18,1024]{3,1,2,0:T(8,128)(2,1)} %copy.45), calls=%async_computation.3 | async-start | bytes 4718592 | tf_op jit(solution)/shard_map/all_to_all | solution.py:42
  518.2 5.2 copy-start.1
Sparse Core Ops, SparseCore 0:
  285.1 26.0 all-gather.3
  381.4 36.1 reduce-scatter.4
  420.4 40.1 reduce-scatter.2

commit v2 on v1

--- a/solution.py
+++ b/solution.py
@@ -1,7 +1,6 @@
 import jax
 import jax.numpy as jnp
 from jax import lax
-from jax.sharding import Mesh
 from jax.sharding import PartitionSpec as P
 
 
@@ -35,20 +34,17 @@
     )
 
 
-def expert_exchange(blocks, rows, cols):
-    capacity, width = blocks.shape[1], blocks.shape[2]
-    blocks = blocks.reshape(rows, cols, capacity, width)
-    blocks = lax.all_to_all(blocks, "ez", 1, 1, tiled=True)
-    blocks = lax.all_to_all(blocks, "ey", 0, 0, tiled=True)
-    return blocks.reshape(rows * cols, capacity, width)
+def expert_exchange(slots, expert_count):
+    slot_total, width = slots.shape
+    blocks = slots.reshape(expert_count, slot_total // expert_count * width // 128, 128)
+    blocks = lax.all_to_all(blocks, "expert", 0, 0, tiled=True)
+    return blocks.reshape(slot_total, width)
 
 
 def on_device(tokens, grad_out, expert_ids, gates, w_in, w_down):
     token_rows, model_width = tokens.shape
     route_width = expert_ids.shape[1]
-    rows = lax.axis_size("ey")
-    cols = lax.axis_size("ez")
-    expert_count = rows * cols
+    expert_count = lax.axis_size("expert")
     route_total = token_rows * route_width
     capacity = route_total // expert_count + max(1, route_total // (8 * expert_count))
     slot_total = expert_count * capacity
@@ -62,20 +58,23 @@
         lower_table, route_marks.astype(jnp.bfloat16), preferred_element_type=jnp.float32
     )
     slot_ranks = jnp.sum((running.astype(jnp.int32) - 1) * route_marks, axis=1)
-    targets = (flat_ids * capacity + slot_ranks).reshape(token_rows, route_width)
+    targets = flat_ids * capacity + slot_ranks
     slot_index = jnp.arange(slot_total, dtype=jnp.int32)
-    slot_hits = targets[None, :, :] == slot_index[:, None, None]
-    slot_of_token = jnp.any(slot_hits, axis=2).astype(jnp.bfloat16)
-    slot_gates = jnp.sum(jnp.where(slot_hits, gates[None, :, :], 0.0), axis=(1, 2))
+    slot_hits = slot_index[:, None] == targets[None, :]
+    slot_gates = jnp.sum(jnp.where(slot_hits, gates.reshape(route_total)[None, :], 0.0), axis=1)
+    token_of_route = (
+        route_index[:, None] // route_width == jnp.arange(token_rows, dtype=jnp.int32)[None, :]
+    ).astype(jnp.bfloat16)
+    slot_of_token = jnp.dot(
+        slot_hits.astype(jnp.bfloat16), token_of_route, preferred_element_type=jnp.float32
+    ).astype(jnp.bfloat16)
     send_tokens = jnp.dot(slot_of_token, tokens, preferred_element_type=jnp.float32).astype(
         jnp.bfloat16
     )
     picked_grads = jnp.dot(slot_of_token, grad_out, preferred_element_type=jnp.float32)
     send_grads = (slot_gates[:, None] * picked_grads).astype(jnp.bfloat16)
     send_both = jnp.concatenate([send_tokens, send_grads], axis=1)
-    recv_both = expert_exchange(
-        send_both.reshape(expert_count, capacity, 2 * model_width), rows, cols
-    ).reshape(slot_total, 2 * model_width)
+    recv_both = expert_exchange(send_both, expert_count)
     slot_tokens = recv_both[:, :model_width]
     slot_grads = recv_both[:, model_width:]
     local_in = w_in[0]
@@ -101,25 +100,16 @@
         scatter_dimension=0,
         tiled=True,
     ).astype(jnp.float32)
-    slot_return = expert_exchange(
-        slot_back.reshape(expert_count, capacity, model_width), rows, cols
-    ).reshape(slot_total, model_width)
+    slot_return = expert_exchange(slot_back, expert_count)
     grad_tokens = contract_first(slot_of_token, slot_return).astype(jnp.bfloat16)
     return (grad_tokens, grad_in_local[None], grad_down_local[None])
 
 
 def solution(mesh):
-    dp_size = mesh.shape["dp"]
-    expert_devices = mesh.devices.reshape(dp_size, -1)
-    rows = 4 if expert_devices.shape[1] % 4 == 0 else 1
-    split_mesh = Mesh(
-        expert_devices.reshape(dp_size, rows, expert_devices.shape[1] // rows),
-        ("dp", "ey", "ez"),
-    )
-    token_spec = P(("dp", "ey", "ez"), None)
-    weight_spec = P(("ey", "ez"), "dp", None)
+    token_spec = P(("dp", "expert"), None)
+    weight_spec = P("expert", "dp", None)
     in_specs = (token_spec, token_spec, token_spec, token_spec, weight_spec, weight_spec)
     out_specs = (token_spec, weight_spec, weight_spec)
     return jax.shard_map(
-        on_device, mesh=split_mesh, in_specs=in_specs, out_specs=out_specs, check_vma=False
+        on_device, mesh=mesh, in_specs=in_specs, out_specs=out_specs, check_vma=False
     )

time: 532 us -> 409 us (0.77)
  blocking collectives: 237 us -> 13.6 us
  waiting for transfers between devices: 152 us -> 292 us
  local copies, waits for them, and re-layouts: 58.2 us -> 31.3 us
  other arithmetic: 20.1 us -> 6.34 us
    all_to_all x1 -> x0, blocking collectives: 224 us -> none  [expert_exchange(): blocks = lax.all_to_all(blocks, 'ez', 1, 1, tiled=True)]
    all_to_all x3 -> x2, waiting for transfers between devices: 152 us -> 217 us  [expert_exchange(): blocks = lax.all_to_all(blocks, 'expert', 0, 0, tiled=True)]
    reduce_scatter x1, waiting for transfers between devices: 0.01 us -> 41.6 us  [on_device(): lax.psum_scatter(contract_first(slot_tokens, pre_grad).astype(jnp.bfloat1...]
    reduce_scatter x1, waiting for transfers between devices: 0.02 us -> 32.2 us  [on_device(): lax.psum_scatter(contract_first(hidden_act, slot_grads).astype(jnp.bfloat...]
    another operation x6 -> x0, local copies, waits for them, and re-layouts: 30.5 us -> none  [the longest x4 20.5 us: expert_exchange(): blocks = blocks.reshape(rows, cols, capacity, width)]
    reshape x0 -> x5, local copies, waits for them, and re-layouts: none -> 21.4 us  [the longest x2 10.7 us: expert_exchange(): slots.reshape(expert_count, slot_total // expert_count * width // 128, 128)]
    all_to_all x4 -> x0, local copies, waits for them, and re-layouts: 18.4 us -> none  [the longest x2 11 us: expert_exchange(): blocks = lax.all_to_all(blocks, 'ey', 0, 0, tiled=True)]
    reduce_sum x1, other arithmetic: 9.34 us -> 0.55 us  [on_device(): jnp.sum(jnp.where(slot_hits, gates.reshape(route_total)[None, :], 0.0), a...]
  transfers between devices with their start and end apart: 6 -> 5, of which waited for: 3 -> 4; matrix products, arithmetic and copies ran while one was open for 6% -> 5% of each run, Pallas kernels for 0% -> 0%
where the time goes in v2:
time: 409 us; the launch traced here: 408 us
  waiting for transfers between devices  292 us (71%)
  local copies, waits for them, and re-layouts  31.3 us (8%)
  starting transfers between devices  26.4 us (6%)
  matrix products  24.9 us (6%)
  between operations  13.9 us (3%)
  blocking collectives  13.6 us (3%)
  other arithmetic  6.34 us (2%)
    all_to_all x2, waiting for transfers between devices, expert_exchange(): blocks = lax.all_to_all(blocks, 'expert', 0, 0, tiled=True)  217 us
    reduce_scatter x1, waiting for transfers between devices, on_device(): lax.psum_scatter(contract_first(slot_tokens, pre_grad).astype(jnp.bfloat1...  41.6 us
    reduce_scatter x1, waiting for transfers between devices, on_device(): lax.psum_scatter(contract_first(hidden_act, slot_grads).astype(jnp.bfloat...  32.2 us
    all_to_all x2, starting transfers between devices, expert_exchange(): blocks = lax.all_to_all(blocks, 'expert', 0, 0, tiled=True)  26.3 us
    all_gather x1, blocking collectives, on_device(): lax.all_gather(local_down, 'dp', axis=0, tiled=True)  13.6 us
    dot_general x3, matrix products, contract_first(): lax.dot_general(left, right, (((0,), (0,)), ((), ())), preferred_element_...  13.3 us
    reshape x2, local copies, waits for them, and re-layouts, expert_exchange(): slots.reshape(expert_count, slot_total // expert_count * width // 128, 128)  10.7 us
    reshape x2, local copies, waits for them, and re-layouts, expert_exchange(): return blocks.reshape(slot_total, width)  10.6 us
  transfers between devices with their start and end apart: 5, of which 4 were waited for; matrix products, arithmetic and copies ran while one was open for 5% of the time, Pallas kernels for 0%

profile of v2, /device:TPU:6, one launch (start us, length us, event | category | flops | bytes accessed | tf_op | source)
XLA Modules:
  0.0 408.3 jit_solution(9145346956681303497)
XLA Ops:
  7.2 0.8 copy.12
  8.1 0.6 fusion.24
  8.7 0.8 copy.13
  9.6 1.0 fusion.3
  10.6 0.6 select_reduce_fusion
  11.2 0.8 convolution_convert_fusion.1
  12.0 0.8 fusion.2
  12.9 2.5 pad_maximum_fusion
  15.4 6.7 %copy.14 = bf16[1152,2048]{1,0:T(8,128)(2,1)} copy(bf16[1152,2048]{0,1:T(8,128)(2,1)} %pad_maximum_fusion) | data formatting | bytes 9437184 | tf_op jit(solution)/shard_map/concatenate | solution.py:76
  22.1 8.3 %reshape.70 = bf16[64,288,128]{2,1,0:T(8,128)(2,1)} reshape(bf16[1152,2048]{1,0:T(8,128)(2,1)} %copy.14) | data formatting | bytes 9437184 | tf_op jit(solution)/shard_map/reshape | solution.py:39
  30.4 19.1 %all-to-all-start = ((bf16[64,288,128]{2,1,0:T(8,128)(2,1)}), bf16[64,288,128]{2,1,0:T(8,128)(2,1)}, u32[]{:S(2)}, u32[]{:S(2)}) async-start(bf16[64,288,128]{2,1,0:T(8,128)(2,1)} %reshape.70), calls=%async_computation | async-start | bytes 9437184 | tf_op jit(solution)/shard_map/all_to_all | solution.py:40
  49.5 0.7 all-gather.4.cloned.1.call-update
  50.2 13.6 %all-gather = bf16[1,384,1024]{2,1,0:T(8,128)(2,1)S(1)} all-gather(bf16[1,48,1024]{2,1,0:T(8,128)(2,1)S(1)} %copy-done.3), channel_id=2, replica_groups=mesh['dp'=8,'expert'=64] {'dp'}, dimensions={1}, use_global_device_ids=true | all-gather | bytes 884736 | tf_op jit(solution)/shard_map/all_gather | solution.py:84
  63.8 196.4 %all-to-all-done = bf16[64,288,128]{2,1,0:T(8,128)(2,1)} async-done(((bf16[64,288,128]{2,1,0:T(8,128)(2,1)}), bf16[64,288,128]{2,1,0:T(8,128)(2,1)}, u32[]{:S(2)}, u32[]{:S(2)}) %all-to-all-start) | async-done | bytes 4718624 | tf_op jit(solution)/shard_map/all_to_all | solution.py:40
  260.1 8.2 %reshape.71 = bf16[1152,2048]{1,0:T(8,128)(2,1)} reshape(bf16[64,288,128]{2,1,0:T(8,128)(2,1)} %all-to-all-done) | data formatting | bytes 9437184 | tf_op jit(solution)/shard_map/reshape | solution.py:41
  268.3 4.6 %fusion.7 = f32[1152,768]{0,1:T(8,128)S(1)} fusion(bf16[1152,2048]{1,0:T(8,128)(2,1)} %reshape.71, bf16[1,1024,768]{2,1,0:T(8,128)(2,1)} %all-gather.4.cloned.1.call-done), kind=kOutput, calls=%fused_computation.14 | convolution fusion | flops 1811939328 | bytes 7471104 | tf_op jit(solution)/shard_map/dot_general | solution.py:86
  273.0 1.6 multiply_convert_fusion.2
  274.6 0.2 copy-done.5
  274.8 1.0 copy-done.6
  275.8 0.3 copy-done.7
  276.1 2.1 convolution_convert_fusion
  278.2 2.4 reshape.72
  280.6 7.2 %all-to-all-start.1 = ((bf16[64,144,128]{2,1,0:T(8,128)(2,1)}), bf16[64,144,128]{2,1,0:T(8,128)(2,1)S(1)}, u32[]{:S(2)}, u32[]{:S(2)}) async-start(bf16[64,144,128]{2,1,0:T(8,128)(2,1)} %reshape.72), calls=%async_computation.1 | async-start | bytes 4718592 | tf_op jit(solution)/shard_map/all_to_all | solution.py:40
  287.8 4.9 %fusion.18 = bf16[384,1024]{1,0:T(8,128)(2,1)} fusion(bf16[1152,2048]{1,0:T(8,128)(2,1)} %reshape.71, f32[1152,768]{0,1:T(8,128)} %copy-done.5), kind=kOutput, calls=%fused_computation.28 | convolution fusion | flops 909017088 | bytes 6684672 | tf_op jit(solution)/shard_map/dot_general | solution.py:26
  292.8 5.5 %fusion.13 = bf16[1024,768]{1,0:T(8,128)(2,1)} fusion(bf16[1152,2048]{1,0:T(8,128)(2,1)} %reshape.71, bf16[1152,384]{0,1:T(8,128)(2,1)} %copy-done.7, bf16[1152,384]{0,1:T(8,128)(2,1)} %copy-done.6), kind=kOutput, calls=%fused_computation.25 | convolution fusion | flops 1816264704 | bytes 5701632 | tf_op jit(solution)/shard_map/dot_general | solution.py:26
  298.3 32.2 %reduce-scatter.5.cloned.1.call-done = bf16[48,1024]{1,0:T(8,128)(2,1)} async-done(((bf16[384,1024]{1,0:T(8,128)(2,1)}), bf16[48,1024]{1,0:T(8,128)(2,1)}) %reduce-scatter.5.cloned.1.call-update) | async-done | bytes 98320 | tf_op jit(solution)/shard_map/reduce_scatter | solution.py:97
  330.6 1.6 bitcast_convert_fusion.1
  332.2 41.6 %reduce-scatter.3.cloned.1.call-done = bf16[128,768]{1,0:T(8,128)(2,1)} async-done(((bf16[1024,768]{1,0:T(8,128)(2,1)}), bf16[128,768]{1,0:T(8,128)(2,1)}) %reduce-scatter.3.cloned.1.call-update) | async-done | bytes 196624 | tf_op jit(solution)/shard_map/reduce_scatter | solution.py:91
  373.7 1.7 bitcast_convert_fusion
  375.4 21.1 %all-to-all-done.1 = bf16[64,144,128]{2,1,0:T(8,128)(2,1)S(1)} async-done(((bf16[64,144,128]{2,1,0:T(8,128)(2,1)}), bf16[64,144,128]{2,1,0:T(8,128)(2,1)S(1)}, u32[]{:S(2)}, u32[]{:S(2)}) %all-to-all-start.1) | async-done | bytes 2359328 | tf_op jit(solution)/shard_map/all_to_all | solution.py:40
  396.5 2.4 reshape.73
  398.9 2.9 convolution_convert_fusion.2
  (22 shorter events, 0.4 us)
Async XLA Ops:
  7.2 4.0 copy-start
  9.6 2.4 copy-start.2
  30.4 19.8 %copy-start.3 = (bf16[1,48,1024]{2,1,0:T(8,128)(2,1)S(1)}, bf16[1,48,1024]{2,1,0:T(8,128)(2,1)}, u32[]{:S(2)}) copy-start(bf16[1,48,1024]{2,1,0:T(8,128)(2,1)} %param.11) | copy-start | bytes 294916
  30.4 229.8 %all-to-all-start = ((bf16[64,288,128]{2,1,0:T(8,128)(2,1)}), bf16[64,288,128]{2,1,0:T(8,128)(2,1)}, u32[]{:S(2)}, u32[]{:S(2)}) async-start(bf16[64,288,128]{2,1,0:T(8,128)(2,1)} %reshape.70), calls=%async_computation | async-start | bytes 9437184 | tf_op jit(solution)/shard_map/all_to_all | solution.py:40
  49.5 218.9 %all-gather.4.cloned.1.call-start = ((), (), s32[]{:S(2)}) async-start(), calls=%async_computation.6 | async-start | bytes 1769472 | tf_op jit(solution)/shard_map/all_gather | solution.py:83
  268.3 4.7 %copy-start.1 = (bf16[1152,2048]{1,0:T(8,128)(2,1)S(1)}, bf16[1152,2048]{1,0:T(8,128)(2,1)}, u32[]{:S(2)}) copy-start(bf16[1152,2048]{1,0:T(8,128)(2,1)} %reshape.71) | copy-start | bytes 14155780
  273.0 1.8 copy-start.5
  273.0 3.1 copy-start.4
  274.8 1.0 copy-start.6
  274.8 1.3 copy-start.7
  280.6 115.9 %all-to-all-start.1 = ((bf16[64,144,128]{2,1,0:T(8,128)(2,1)}), bf16[64,144,128]{2,1,0:T(8,128)(2,1)S(1)}, u32[]{:S(2)}, u32[]{:S(2)}) async-start(bf16[64,144,128]{2,1,0:T(8,128)(2,1)} %reshape.72), calls=%async_computation.1 | async-start | bytes 4718592 | tf_op jit(solution)/shard_map/all_to_all | solution.py:40
  287.8 42.8 %reduce-scatter.5.cloned.1.call-start = ((), (), s32[]{:S(2)}) async-start(), calls=%async_computation.5 | async-start | bytes 884736 | tf_op jit(solution)/shard_map/reduce_scatter | solution.py:97
  292.7 81.0 %reduce-scatter.3.cloned.1.call-start = ((), (), s32[]{:S(2)}) async-start(), calls=%async_computation.4 | async-start | bytes 1769472 | tf_op jit(solution)/shard_map/reduce_scatter | solution.py:91
Sparse Core Ops, SparseCore 0:
  52.4 31.0 all-gather.3
  292.8 37.6 reduce-scatter.4
  333.4 40.2 reduce-scatter.2

commit v3 on v2

--- a/solution.py
+++ b/solution.py
@@ -35,10 +35,10 @@
 
 
 def expert_exchange(slots, expert_count):
-    slot_total, width = slots.shape
-    blocks = slots.reshape(expert_count, slot_total // expert_count * width // 128, 128)
+    slot_total, chunks, lanes = slots.shape
+    blocks = slots.reshape(expert_count, slot_total // expert_count * chunks, lanes)
     blocks = lax.all_to_all(blocks, "expert", 0, 0, tiled=True)
-    return blocks.reshape(slot_total, width)
+    return blocks.reshape(slot_total, chunks, lanes)
 
 
 def on_device(tokens, grad_out, expert_ids, gates, w_in, w_down):
@@ -68,15 +68,24 @@
     slot_of_token = jnp.dot(
         slot_hits.astype(jnp.bfloat16), token_of_route, preferred_element_type=jnp.float32
     ).astype(jnp.bfloat16)
-    send_tokens = jnp.dot(slot_of_token, tokens, preferred_element_type=jnp.float32).astype(
-        jnp.bfloat16
+    chunks = model_width // 128
+    send_tokens = lax.dot_general(
+        slot_of_token,
+        tokens.reshape(token_rows, chunks, 128),
+        (((1,), (0,)), ((), ())),
+        preferred_element_type=jnp.float32,
+    ).astype(jnp.bfloat16)
+    picked_grads = lax.dot_general(
+        slot_of_token,
+        grad_out.reshape(token_rows, chunks, 128),
+        (((1,), (0,)), ((), ())),
+        preferred_element_type=jnp.float32,
     )
-    picked_grads = jnp.dot(slot_of_token, grad_out, preferred_element_type=jnp.float32)
-    send_grads = (slot_gates[:, None] * picked_grads).astype(jnp.bfloat16)
+    send_grads = (slot_gates[:, None, None] * picked_grads).astype(jnp.bfloat16)
     send_both = jnp.concatenate([send_tokens, send_grads], axis=1)
     recv_both = expert_exchange(send_both, expert_count)
-    slot_tokens = recv_both[:, :model_width]
-    slot_grads = recv_both[:, model_width:]
+    slot_tokens = recv_both[:, :chunks, :].reshape(slot_total, model_width)
+    slot_grads = recv_both[:, chunks:, :].reshape(slot_total, model_width)
     local_in = w_in[0]
     local_down = w_down[0]
     full_in, full_down = (
@@ -86,7 +95,12 @@
     preact = jnp.dot(slot_tokens, full_in, preferred_element_type=jnp.float32)
     grad_hidden = contract_last(slot_grads, full_down)
     pre_grad = pre_grads(preact, grad_hidden)
-    slot_back = contract_last(pre_grad, full_in).astype(jnp.bfloat16)
+    slot_back = lax.dot_general(
+        pre_grad,
+        full_in.reshape(chunks, 128, full_in.shape[1]),
+        (((1,), (2,)), ((), ())),
+        preferred_element_type=jnp.float32,
+    ).astype(jnp.bfloat16)
     hidden_act = hidden_from(preact)
     grad_in_local = lax.psum_scatter(
         contract_first(slot_tokens, pre_grad).astype(jnp.bfloat16),
@@ -101,7 +115,11 @@
         tiled=True,
     ).astype(jnp.float32)
     slot_return = expert_exchange(slot_back, expert_count)
-    grad_tokens = contract_first(slot_of_token, slot_return).astype(jnp.bfloat16)
+    grad_tokens = (
+        contract_first(slot_of_token, slot_return)
+        .astype(jnp.bfloat16)
+        .reshape(token_rows, model_width)
+    )
     return (grad_tokens, grad_in_local[None], grad_down_local[None])
 
 

time: 409 us -> 407 us (level)
    reshape x4 -> x1, local copies, waits for them, and re-layouts: 21.3 us -> 3.23 us  [expert_exchange(): return blocks.reshape(slot_total, chunks, lanes)]
    convert_element_type x0 -> x1, local copies, waits for them, and re-layouts: none -> 7.74 us  [on_device(): slot_back = lax.dot_general(pre_grad, full_in.reshape(chunks, 128, full_i...]
    concatenate x1, local copies, waits for them, and re-layouts: 6.71 us -> 14.2 us  [on_device(): send_both = jnp.concatenate([send_tokens, send_grads], axis=1)]
    dot_general x3 -> x2, matrix products: 13.3 us -> 10.5 us  [contract_first(): lax.dot_general(left, right, (((0,), (0,)), ((), ())), preferred_element_...]
  transfers between devices with their start and end apart: 5 -> 5, of which waited for: 4 -> 4; matrix products, arithmetic and copies ran while one was open for 5% -> 4% of each run, Pallas kernels for 0% -> 0%
where the time goes in v3:
time: 407 us
  waiting for transfers between devices  291 us (71%)
  local copies, waits for them, and re-layouts  33.7 us (8%)
  starting transfers between devices  26.6 us (7%)
  matrix products  23 us (6%)
  blocking collectives  14.6 us (4%)
  between operations  14 us (3%)
  other arithmetic  4.29 us (1%)
    all_to_all x2, waiting for transfers between devices, expert_exchange(): blocks = lax.all_to_all(blocks, 'expert', 0, 0, tiled=True)  216 us
    reduce_scatter x1, waiting for transfers between devices, on_device(): lax.psum_scatter(contract_first(slot_tokens, pre_grad).astype(jnp.bfloat1...  41.5 us
    reduce_scatter x1, waiting for transfers between devices, on_device(): lax.psum_scatter(contract_first(hidden_act, slot_grads).astype(jnp.bfloat...  32 us
    all_to_all x2, starting transfers between devices, expert_exchange(): blocks = lax.all_to_all(blocks, 'expert', 0, 0, tiled=True)  26.3 us
    all_gather x1, blocking collectives, on_device(): lax.all_gather(local_down, 'dp', axis=0, tiled=True)  14.6 us
    concatenate x1, local copies, waits for them, and re-layouts, on_device(): send_both = jnp.concatenate([send_tokens, send_grads], axis=1)  14.2 us
    dot_general x2, matrix products, contract_first(): lax.dot_general(left, right, (((0,), (0,)), ((), ())), preferred_element_...  10.5 us
  transfers between devices with their start and end apart: 5, of which 4 were waited for; matrix products, arithmetic and copies ran while one was open for 4% of the time, Pallas kernels for 0%

profile of v3, /device:TPU:6, one launch (start us, length us, event | category | flops | bytes accessed | tf_op | source)
XLA Modules:
  0.0 406.8 jit_solution(3373076025676624003)
XLA Ops:
  7.2 0.8 copy.22
  8.1 0.6 fusion.28
  8.7 0.8 copy.24
  9.6 1.0 fusion.3
  10.6 0.6 select_reduce_fusion
  11.2 0.8 convolution_convert_fusion.1
  12.0 0.8 fusion.2
  12.7 0.4 pad_maximum_fusion
  13.1 14.2 %copy.26 = bf16[1152,16,128]{2,1,0:T(8,128)(2,1)} copy(bf16[1152,16,128]{2,0,1:T(8,128)(2,1)S(1)} %pad_maximum_fusion) | data formatting | bytes 9437184 | tf_op jit(solution)/shard_map/concatenate | solution.py:85
  27.3 19.1 %all-to-all-start = ((bf16[64,288,128]{2,1,0:T(8,128)(2,1)}), bf16[64,288,128]{2,1,0:T(8,128)(2,1)}, u32[]{:S(2)}, u32[]{:S(2)}) async-start(bf16[64,288,128]{2,1,0:T(8,128)(2,1)} %bitcast.65), calls=%async_computation | async-start | bytes 9437184 | tf_op jit(solution)/shard_map/all_to_all | solution.py:40
  46.5 0.7 all-gather.4.cloned.1.call-update
  47.2 14.6 %all-gather = bf16[1,384,1024]{2,1,0:T(8,128)(2,1)} all-gather(bf16[1,48,1024]{2,1,0:T(8,128)(2,1)S(1)} %copy-done.6), channel_id=2, replica_groups=mesh['dp'=8,'expert'=64] {'dp'}, dimensions={1}, use_global_device_ids=true | all-gather | bytes 884736 | tf_op jit(solution)/shard_map/all_gather | solution.py:93
  61.8 195.3 %all-to-all-done = bf16[64,288,128]{2,1,0:T(8,128)(2,1)} async-done(((bf16[64,288,128]{2,1,0:T(8,128)(2,1)}), bf16[64,288,128]{2,1,0:T(8,128)(2,1)}, u32[]{:S(2)}, u32[]{:S(2)}) %all-to-all-start) | async-done | bytes 4718624 | tf_op jit(solution)/shard_map/all_to_all | solution.py:40
  257.1 3.5 fusion.45
  260.7 4.6 %fusion.6 = f32[1152,768]{0,1:T(8,128)S(1)} fusion(bf16[144,8,8,128]{3,2,1,0:T(8,128)(2,1)S(1)} %bitcast.70, bf16[1,1024,768]{2,1,0:T(8,128)(2,1)} %all-gather.4.cloned.1.call-done), kind=kOutput, calls=%fused_computation.13 | convolution fusion | flops 1811939328 | bytes 7471104 | tf_op jit(solution)/shard_map/dot_general | solution.py:95
  265.4 1.7 multiply_convert_fusion.2
  267.2 0.7 copy-done.7
  267.9 2.3 convolution_convert_fusion
  270.2 7.7 %copy.28 = bf16[1152,8,128]{2,1,0:T(8,128)(2,1)} copy(bf16[1152,8,128]{2,0,1:T(8,128)(2,1)S(1)} %convolution_convert_fusion) | data formatting | bytes 4718592 | tf_op jit(solution)/shard_map/convert_element_type | solution.py:103
  278.0 7.2 %all-to-all-start.1 = ((bf16[64,144,128]{2,1,0:T(8,128)(2,1)}), bf16[64,144,128]{2,1,0:T(8,128)(2,1)S(1)}, u32[]{:S(2)}, u32[]{:S(2)}) async-start(bf16[64,144,128]{2,1,0:T(8,128)(2,1)} %bitcast.68), calls=%async_computation.1 | async-start | bytes 4718592 | tf_op jit(solution)/shard_map/all_to_all | solution.py:40
  285.2 4.9 %fusion.22 = bf16[384,1024]{1,0:T(8,128)(2,1)} fusion(bf16[144,8,8,128]{3,2,1,0:T(8,128)(2,1)} %bitcast.72, f32[1152,768]{0,1:T(8,128)} %copy-done.8), kind=kOutput, calls=%fused_computation.32 | convolution fusion | flops 909017088 | bytes 6684672 | tf_op jit(solution)/shard_map/dot_general | solution.py:26
  290.1 0.3 reduce-scatter.3.cloned.1.call-start
  290.4 5.6 %fusion.18 = bf16[1024,768]{1,0:T(8,128)(2,1)} fusion(bf16[144,8,8,128]{3,2,1,0:T(8,128)(2,1)} %bitcast.71, bf16[1152,384]{0,1:T(8,128)(2,1)} %copy-done.10, bf16[1152,384]{0,1:T(8,128)(2,1)} %copy-done.9), kind=kOutput, calls=%fused_computation.30 | convolution fusion | flops 1816264704 | bytes 5701632 | tf_op jit(solution)/shard_map/dot_general | solution.py:26
  296.0 32.0 %reduce-scatter.5.cloned.1.call-done = bf16[48,1024]{1,0:T(8,128)(2,1)} async-done(((bf16[384,1024]{1,0:T(8,128)(2,1)}), bf16[48,1024]{1,0:T(8,128)(2,1)}) %reduce-scatter.5.cloned.1.call-update) | async-done | bytes 98320 | tf_op jit(solution)/shard_map/reduce_scatter | solution.py:111
  328.1 1.6 bitcast_convert_fusion.1
  329.7 41.5 %reduce-scatter.3.cloned.1.call-done = bf16[128,768]{1,0:T(8,128)(2,1)} async-done(((bf16[1024,768]{1,0:T(8,128)(2,1)}), bf16[128,768]{1,0:T(8,128)(2,1)}) %reduce-scatter.3.cloned.1.call-update) | async-done | bytes 196624 | tf_op jit(solution)/shard_map/reduce_scatter | solution.py:105
  371.1 1.7 bitcast_convert_fusion
  372.8 21.0 %all-to-all-done.1 = bf16[64,144,128]{2,1,0:T(8,128)(2,1)S(1)} async-done(((bf16[64,144,128]{2,1,0:T(8,128)(2,1)}), bf16[64,144,128]{2,1,0:T(8,128)(2,1)S(1)}, u32[]{:S(2)}, u32[]{:S(2)}) %all-to-all-start.1) | async-done | bytes 2359328 | tf_op jit(solution)/shard_map/all_to_all | solution.py:40
  393.9 1.4 copy-done.1
  395.3 3.2 copy.29
  398.6 0.8 fusion.46
  399.4 0.8 copy.30
  (29 shorter events, 0.5 us)
Async XLA Ops:
  7.2 4.0 copy-start
  9.6 2.3 copy-start.5
  27.3 19.8 %copy-start.6 = (bf16[1,48,1024]{2,1,0:T(8,128)(2,1)S(1)}, bf16[1,48,1024]{2,1,0:T(8,128)(2,1)}, u32[]{:S(2)}) copy-start(bf16[1,48,1024]{2,1,0:T(8,128)(2,1)} %param.11) | copy-start | bytes 294916
  27.3 229.8 %all-to-all-start = ((bf16[64,288,128]{2,1,0:T(8,128)(2,1)}), bf16[64,288,128]{2,1,0:T(8,128)(2,1)}, u32[]{:S(2)}, u32[]{:S(2)}) async-start(bf16[64,288,128]{2,1,0:T(8,128)(2,1)} %bitcast.65), calls=%async_computation | async-start | bytes 9437184 | tf_op jit(solution)/shard_map/all_to_all | solution.py:40
  46.4 214.2 %all-gather.4.cloned.1.call-start = ((), (), s32[]{:S(2)}) async-start(), calls=%async_computation.6 | async-start | bytes 1769472 | tf_op jit(solution)/shard_map/all_gather | solution.py:92
  260.6 4.7 %copy-start.2 = (bf16[1152,8,128]{2,1,0:T(8,128)(2,1)}, bf16[1152,8,128]{2,1,0:T(8,128)(2,1)S(1)}, u32[]{:S(2)}) copy-start(bf16[1152,8,128]{2,1,0:T(8,128)(2,1)S(1)} %get-tuple-element.14) | copy-start | bytes 7077892
  260.6 4.7 %copy-start.3 = (bf16[1152,8,128]{2,1,0:T(8,128)(2,1)S(1)}, bf16[1152,8,128]{2,1,0:T(8,128)(2,1)}, u32[]{:S(2)}) copy-start(bf16[1152,8,128]{2,1,0:T(8,128)(2,1)} %get-tuple-element.15) | copy-start | bytes 7077892
  260.6 4.7 %copy-start.4 = (bf16[1,384,1024]{2,1,0:T(8,128)(2,1)S(1)}, bf16[1,384,1024]{2,1,0:T(8,128)(2,1)}, u32[]{:S(2)}) copy-start(bf16[1,384,1024]{2,1,0:T(8,128)(2,1)} %all-gather) | copy-start | bytes 2359300
  265.3 1.9 copy-start.8
  265.4 2.6 copy-start.7
  267.2 3.0 copy-start.9
  267.2 3.1 copy-start.10
  278.0 115.9 %all-to-all-start.1 = ((bf16[64,144,128]{2,1,0:T(8,128)(2,1)}), bf16[64,144,128]{2,1,0:T(8,128)(2,1)S(1)}, u32[]{:S(2)}, u32[]{:S(2)}) async-start(bf16[64,144,128]{2,1,0:T(8,128)(2,1)} %bitcast.68), calls=%async_computation.1 | async-start | bytes 4718592 | tf_op jit(solution)/shard_map/all_to_all | solution.py:40
  285.2 42.9 %reduce-scatter.5.cloned.1.call-start = ((), (), s32[]{:S(2)}) async-start(), calls=%async_computation.5 | async-start | bytes 884736 | tf_op jit(solution)/shard_map/reduce_scatter | solution.py:111
  290.1 81.0 %reduce-scatter.3.cloned.1.call-start = ((), (), s32[]{:S(2)}) async-start(), calls=%async_computation.4 | async-start | bytes 1769472 | tf_op jit(solution)/shard_map/reduce_scatter | solution.py:105
  393.9 1.4 copy-start.1
Sparse Core Ops, SparseCore 0:
  49.4 31.0 all-gather.3
  290.3 37.7 reduce-scatter.4
  330.9 40.1 reduce-scatter.2

commit v4 on v3

--- a/solution.py
+++ b/solution.py
@@ -69,20 +69,16 @@
         slot_hits.astype(jnp.bfloat16), token_of_route, preferred_element_type=jnp.float32
     ).astype(jnp.bfloat16)
     chunks = model_width // 128
-    send_tokens = lax.dot_general(
-        slot_of_token,
-        tokens.reshape(token_rows, chunks, 128),
-        (((1,), (0,)), ((), ())),
-        preferred_element_type=jnp.float32,
-    ).astype(jnp.bfloat16)
-    picked_grads = lax.dot_general(
-        slot_of_token,
-        grad_out.reshape(token_rows, chunks, 128),
-        (((1,), (0,)), ((), ())),
-        preferred_element_type=jnp.float32,
+    both_rows = jnp.concatenate(
+        [tokens.reshape(token_rows, chunks, 128), grad_out.reshape(token_rows, chunks, 128)],
+        axis=1,
     )
-    send_grads = (slot_gates[:, None, None] * picked_grads).astype(jnp.bfloat16)
-    send_both = jnp.concatenate([send_tokens, send_grads], axis=1)
+    picked = lax.dot_general(
+        slot_of_token, both_rows, (((1,), (0,)), ((), ())), preferred_element_type=jnp.float32
+    )
+    chunk_index = jnp.arange(2 * chunks, dtype=jnp.int32)[None, :, None]
+    row_scale = jnp.where(chunk_index < chunks, jnp.ones((), jnp.float32), slot_gates[:, None, None])
+    send_both = (row_scale * picked).astype(jnp.bfloat16)
     recv_both = expert_exchange(send_both, expert_count)
     slot_tokens = recv_both[:, :chunks, :].reshape(slot_total, model_width)
     slot_grads = recv_both[:, chunks:, :].reshape(slot_total, model_width)
@@ -95,12 +91,9 @@
     preact = jnp.dot(slot_tokens, full_in, preferred_element_type=jnp.float32)
     grad_hidden = contract_last(slot_grads, full_down)
     pre_grad = pre_grads(preact, grad_hidden)
-    slot_back = lax.dot_general(
-        pre_grad,
-        full_in.reshape(chunks, 128, full_in.shape[1]),
-        (((1,), (2,)), ((), ())),
-        preferred_element_type=jnp.float32,
-    ).astype(jnp.bfloat16)
+    slot_back = (
+        contract_last(pre_grad, full_in).astype(jnp.bfloat16).reshape(slot_total, chunks, 128)
+    )
     hidden_act = hidden_from(preact)
     grad_in_local = lax.psum_scatter(
         contract_first(slot_tokens, pre_grad).astype(jnp.bfloat16),

time: 407 us -> 404 us (level)
  local copies, waits for them, and re-layouts: 33.7 us -> 29.6 us
    concatenate x1 -> x0, local copies, waits for them, and re-layouts: 14.2 us -> none  [on_device(): send_both = jnp.concatenate([send_tokens, send_grads], axis=1)]
    convert_element_type x1, local copies, waits for them, and re-layouts: 7.74 us -> 14.1 us  [on_device(): send_both = (row_scale * picked).astype(jnp.bfloat16)]
where the time goes in v4:
time: 404 us; the launch traced here: 403 us
  waiting for transfers between devices  292 us (72%)
  local copies, waits for them, and re-layouts  29.6 us (7%)
  starting transfers between devices  26.6 us (7%)
  matrix products  23.9 us (6%)
  between operations  14 us (3%)
  blocking collectives  13.6 us (3%)
    all_to_all x2, waiting for transfers between devices, expert_exchange(): blocks = lax.all_to_all(blocks, 'expert', 0, 0, tiled=True)  217 us
    reduce_scatter x1, waiting for transfers between devices, on_device(): lax.psum_scatter(contract_first(slot_tokens, pre_grad).astype(jnp.bfloat1...  41.4 us
    reduce_scatter x1, waiting for transfers between devices, on_device(): lax.psum_scatter(contract_first(hidden_act, slot_grads).astype(jnp.bfloat...  32.3 us
    all_to_all x2, starting transfers between devices, expert_exchange(): blocks = lax.all_to_all(blocks, 'expert', 0, 0, tiled=True)  26.3 us
    convert_element_type x1, local copies, waits for them, and re-layouts, on_device(): send_both = (row_scale * picked).astype(jnp.bfloat16)  14.1 us
    all_gather x1, blocking collectives, on_device(): lax.all_gather(local_down, 'dp', axis=0, tiled=True)  13.6 us
    dot_general x2, matrix products, contract_first(): lax.dot_general(left, right, (((0,), (0,)), ((), ())), preferred_element_...  10.3 us
  transfers between devices with their start and end apart: 5, of which 4 were waited for; matrix products, arithmetic and copies ran while one was open for 4% of the time, Pallas kernels for 0%

profile of v4, /device:TPU:6, one launch (start us, length us, event | category | flops | bytes accessed | tf_op | source)
XLA Modules:
  0.0 403.4 jit_solution(281320189677718888)
XLA Ops:
  7.2 0.8 copy.19
  8.1 0.6 fusion.27
  8.7 0.8 copy.20
  9.6 1.0 fusion.2
  10.6 0.6 select_reduce_fusion
  11.4 0.2 copy.23
  12.0 2.8 multiply_convert_fusion
  14.8 14.1 %copy.25 = bf16[1152,16,128]{2,1,0:T(8,128)(2,1)} copy(bf16[1152,16,128]{2,0,1:T(8,128)(2,1)S(1)} %multiply_convert_fusion) | data formatting | bytes 9437184 | tf_op jit(solution)/shard_map/convert_element_type | solution.py:81
  29.0 19.1 %all-to-all-start = ((bf16[64,288,128]{2,1,0:T(8,128)(2,1)}), bf16[64,288,128]{2,1,0:T(8,128)(2,1)}, u32[]{:S(2)}, u32[]{:S(2)}) async-start(bf16[64,288,128]{2,1,0:T(8,128)(2,1)} %bitcast.47), calls=%async_computation | async-start | bytes 9437184 | tf_op jit(solution)/shard_map/all_to_all | solution.py:40
  48.1 0.7 all-gather.4.cloned.1.call-update
  48.8 13.6 %all-gather = bf16[1,384,1024]{2,1,0:T(8,128)(2,1)S(1)} all-gather(bf16[1,48,1024]{2,1,0:T(8,128)(2,1)S(1)} %copy-done.5), channel_id=2, replica_groups=mesh['dp'=8,'expert'=64] {'dp'}, dimensions={1}, use_global_device_ids=true | all-gather | bytes 884736 | tf_op jit(solution)/shard_map/all_gather | solution.py:89
  62.4 196.4 %all-to-all-done = bf16[64,288,128]{2,1,0:T(8,128)(2,1)} async-done(((bf16[64,288,128]{2,1,0:T(8,128)(2,1)}), bf16[64,288,128]{2,1,0:T(8,128)(2,1)}, u32[]{:S(2)}, u32[]{:S(2)}) %all-to-all-start) | async-done | bytes 4718624 | tf_op jit(solution)/shard_map/all_to_all | solution.py:40
  258.8 3.5 fusion.43
  262.3 4.7 %fusion.5 = f32[1152,768]{0,1:T(8,128)S(1)} fusion(bf16[144,8,8,128]{3,2,1,0:T(8,128)(2,1)S(1)} %bitcast.51, bf16[1,1024,768]{2,1,0:T(8,128)(2,1)} %all-gather.4.cloned.1.call-done), kind=kOutput, calls=%fused_computation.10 | convolution fusion | flops 1811939328 | bytes 7471104 | tf_op jit(solution)/shard_map/dot_general | solution.py:91
  267.0 1.7 multiply_convert_fusion.3
  268.8 1.0 copy-done.8
  269.8 0.3 copy-done.10
  270.1 2.1 convolution_convert_fusion
  272.2 2.4 reshape_reshape.3
  274.6 7.2 %all-to-all-start.1 = ((bf16[64,144,128]{2,1,0:T(8,128)(2,1)}), bf16[64,144,128]{2,1,0:T(8,128)(2,1)S(1)}, u32[]{:S(2)}, u32[]{:S(2)}) async-start(bf16[64,144,128]{2,1,0:T(8,128)(2,1)} %reshape_reshape.3), calls=%async_computation.1 | async-start | bytes 4718592 | tf_op jit(solution)/shard_map/all_to_all | solution.py:40
  281.9 5.0 %fusion.21 = bf16[384,1024]{1,0:T(8,128)(2,1)} fusion(bf16[144,8,8,128]{3,2,1,0:T(8,128)(2,1)} %bitcast.53, f32[1152,768]{0,1:T(8,128)} %copy-done.7), kind=kOutput, calls=%fused_computation.29 | convolution fusion | flops 909017088 | bytes 6684672 | tf_op jit(solution)/shard_map/dot_general | solution.py:26
  286.9 0.3 reduce-scatter.3.cloned.1.call-start
  287.2 5.3 %fusion.16 = bf16[1024,768]{1,0:T(8,128)(2,1)} fusion(bf16[144,8,8,128]{3,2,1,0:T(8,128)(2,1)} %bitcast.52, bf16[1152,384]{0,1:T(8,128)(2,1)} %copy-done.10, bf16[1152,384]{0,1:T(8,128)(2,1)S(1)} %copy-done.9), kind=kOutput, calls=%fused_computation.26 | convolution fusion | flops 1816264704 | bytes 5701632 | tf_op jit(solution)/shard_map/dot_general | solution.py:26
  292.5 32.3 %reduce-scatter.5.cloned.1.call-done = bf16[48,1024]{1,0:T(8,128)(2,1)} async-done(((bf16[384,1024]{1,0:T(8,128)(2,1)}), bf16[48,1024]{1,0:T(8,128)(2,1)}) %reduce-scatter.5.cloned.1.call-update) | async-done | bytes 98320 | tf_op jit(solution)/shard_map/reduce_scatter | solution.py:104
  324.8 1.6 bitcast_convert_fusion.1
  326.4 41.4 %reduce-scatter.3.cloned.1.call-done = bf16[128,768]{1,0:T(8,128)(2,1)} async-done(((bf16[1024,768]{1,0:T(8,128)(2,1)}), bf16[128,768]{1,0:T(8,128)(2,1)}) %reduce-scatter.3.cloned.1.call-update) | async-done | bytes 196624 | tf_op jit(solution)/shard_map/reduce_scatter | solution.py:98
  367.8 1.7 bitcast_convert_fusion
  369.5 21.0 %all-to-all-done.1 = bf16[64,144,128]{2,1,0:T(8,128)(2,1)S(1)} async-done(((bf16[64,144,128]{2,1,0:T(8,128)(2,1)}), bf16[64,144,128]{2,1,0:T(8,128)(2,1)S(1)}, u32[]{:S(2)}, u32[]{:S(2)}) %all-to-all-start.1) | async-done | bytes 2359328 | tf_op jit(solution)/shard_map/all_to_all | solution.py:40
  390.5 1.4 copy-done
  392.0 3.2 copy.26
  395.2 0.8 fusion.44
  396.0 0.9 copy.27
  (33 shorter events, 1.1 us)
Async XLA Ops:
  7.2 4.0 copy-start.3
  8.1 3.4 copy-start.4
  29.0 19.9 %copy-start.5 = (bf16[1,48,1024]{2,1,0:T(8,128)(2,1)S(1)}, bf16[1,48,1024]{2,1,0:T(8,128)(2,1)}, u32[]{:S(2)}) copy-start(bf16[1,48,1024]{2,1,0:T(8,128)(2,1)} %param.11) | copy-start | bytes 294916
  29.0 229.8 %all-to-all-start = ((bf16[64,288,128]{2,1,0:T(8,128)(2,1)}), bf16[64,288,128]{2,1,0:T(8,128)(2,1)}, u32[]{:S(2)}, u32[]{:S(2)}) async-start(bf16[64,288,128]{2,1,0:T(8,128)(2,1)} %bitcast.47), calls=%async_computation | async-start | bytes 9437184 | tf_op jit(solution)/shard_map/all_to_all | solution.py:40
  48.1 214.2 %all-gather.4.cloned.1.call-start = ((), (), s32[]{:S(2)}) async-start(), calls=%async_computation.6 | async-start | bytes 1769472 | tf_op jit(solution)/shard_map/all_gather | solution.py:88
  262.3 4.7 %copy-start.1 = (bf16[1152,8,128]{2,1,0:T(8,128)(2,1)}, bf16[1152,8,128]{2,1,0:T(8,128)(2,1)S(1)}, u32[]{:S(2)}) copy-start(bf16[1152,8,128]{2,1,0:T(8,128)(2,1)S(1)} %get-tuple-element.14) | copy-start | bytes 7077892
  262.3 4.7 %copy-start.2 = (bf16[1152,8,128]{2,1,0:T(8,128)(2,1)S(1)}, bf16[1152,8,128]{2,1,0:T(8,128)(2,1)}, u32[]{:S(2)}) copy-start(bf16[1152,8,128]{2,1,0:T(8,128)(2,1)} %get-tuple-element.15) | copy-start | bytes 7077892
  266.9 1.9 copy-start.7
  267.0 3.2 copy-start.6
  268.8 1.0 copy-start.8
  268.8 1.3 copy-start.10
  274.6 115.9 %all-to-all-start.1 = ((bf16[64,144,128]{2,1,0:T(8,128)(2,1)}), bf16[64,144,128]{2,1,0:T(8,128)(2,1)S(1)}, u32[]{:S(2)}, u32[]{:S(2)}) async-start(bf16[64,144,128]{2,1,0:T(8,128)(2,1)} %reshape_reshape.3), calls=%async_computation.1 | async-start | bytes 4718592 | tf_op jit(solution)/shard_map/all_to_all | solution.py:40
  281.8 5.3 %copy-start.9 = (bf16[1152,384]{0,1:T(8,128)(2,1)S(1)}, bf16[1152,384]{0,1:T(8,128)(2,1)}, u32[]{:S(2)}) copy-start(bf16[1152,384]{0,1:T(8,128)(2,1)} %copy-done.8) | copy-start | bytes 2654212
  281.8 43.0 %reduce-scatter.5.cloned.1.call-start = ((), (), s32[]{:S(2)}) async-start(), calls=%async_computation.5 | async-start | bytes 884736 | tf_op jit(solution)/shard_map/reduce_scatter | solution.py:104
  286.9 80.9 %reduce-scatter.3.cloned.1.call-start = ((), (), s32[]{:S(2)}) async-start(), calls=%async_computation.4 | async-start | bytes 1769472 | tf_op jit(solution)/shard_map/reduce_scatter | solution.py:98
  390.5 1.4 copy-start
Sparse Core Ops, SparseCore 0:
  51.0 31.0 all-gather.3
  287.0 37.7 reduce-scatter.4
  327.6 40.1 reduce-scatter.2

commit v5 on v4

--- a/solution.py
+++ b/solution.py
@@ -73,11 +73,12 @@
         [tokens.reshape(token_rows, chunks, 128), grad_out.reshape(token_rows, chunks, 128)],
         axis=1,
     )
-    picked = lax.dot_general(
-        slot_of_token, both_rows, (((1,), (0,)), ((), ())), preferred_element_type=jnp.float32
-    )
+    slot_routes = jnp.sum(jnp.where(slot_hits, route_index[None, :], 0), axis=1)
+    occupied = jnp.any(slot_hits, axis=1)
+    picked = both_rows[slot_routes // route_width].astype(jnp.float32)
     chunk_index = jnp.arange(2 * chunks, dtype=jnp.int32)[None, :, None]
     row_scale = jnp.where(chunk_index < chunks, jnp.ones((), jnp.float32), slot_gates[:, None, None])
+    row_scale = jnp.where(occupied[:, None, None], row_scale, jnp.zeros((), jnp.float32))
     send_both = (row_scale * picked).astype(jnp.bfloat16)
     recv_both = expert_exchange(send_both, expert_count)
     slot_tokens = recv_both[:, :chunks, :].reshape(slot_total, model_width)

time: 404 us -> 400 us (0.990)
  local copies, waits for them, and re-layouts: 29.6 us -> 18.8 us
  other arithmetic: 3.96 us -> 11.5 us
    convert_element_type x1 -> x0, local copies, waits for them, and re-layouts: 14.1 us -> none  [on_device(): send_both = (row_scale * picked).astype(jnp.bfloat16)]
    convert_element_type x0 -> x1, other arithmetic: none -> 6.26 us  [on_device(): send_both = (row_scale * picked).astype(jnp.bfloat16)]
    gather x0 -> x1, local copies, waits for them, and re-layouts: none -> 4.84 us  [on_device(): picked = both_rows[slot_routes // route_width].astype(jnp.float32)]
where the time goes in v5:
time: 400 us
  waiting for transfers between devices  292 us (73%)
  starting transfers between devices  26.6 us (7%)
  matrix products  23.7 us (6%)
  local copies, waits for them, and re-layouts  18.8 us (5%)
  between operations  14 us (4%)
  blocking collectives  13.6 us (3%)
  other arithmetic  11.5 us (3%)
    all_to_all x2, waiting for transfers between devices, expert_exchange(): blocks = lax.all_to_all(blocks, 'expert', 0, 0, tiled=True)  217 us
    reduce_scatter x1, waiting for transfers between devices, on_device(): lax.psum_scatter(contract_first(slot_tokens, pre_grad).astype(jnp.bfloat1...  41.4 us
    reduce_scatter x1, waiting for transfers between devices, on_device(): lax.psum_scatter(contract_first(hidden_act, slot_grads).astype(jnp.bfloat...  32.1 us
    all_to_all x2, starting transfers between devices, expert_exchange(): blocks = lax.all_to_all(blocks, 'expert', 0, 0, tiled=True)  26.3 us
    all_gather x1, blocking collectives, on_device(): lax.all_gather(local_down, 'dp', axis=0, tiled=True)  13.6 us
    dot_general x2, matrix products, contract_first(): lax.dot_general(left, right, (((0,), (0,)), ((), ())), preferred_element_...  10.5 us
  transfers between devices with their start and end apart: 5, of which 4 were waited for; matrix products, arithmetic and copies ran while one was open for 4% of the time, Pallas kernels for 0%

profile of v5, /device:TPU:6, one launch (start us, length us, event | category | flops | bytes accessed | tf_op | source)
XLA Modules:
  0.0 399.7 jit_solution(4009378944013035038)
XLA Ops:
  7.2 0.8 copy.18
  8.1 0.6 fusion.30
  8.7 0.6 fusion.1
  9.4 0.6 select_reduce_fusion
  10.2 0.8 copy.20
  11.1 0.6 select_reduce_fusion.1
  11.9 0.3 broadcast_in_dim.96
  12.7 4.8 %gather_fusion = bf16[1152,16,128]{2,1,0:T(8,128)(2,1)} fusion(bf16[128,16,128]{2,1,0:T(8,128)(2,1)S(1)} %pad_maximum_fusion.3, s32[2048]{0:T(1024)S(1)} %pad_clamp_fusion), kind=kCustom, calls=%fused_computation | custom fusion | bytes 9441792 | tf_op jit(solution)/shard_map/gather | solution.py:78
  17.5 6.3 %fusion = bf16[64,288,128]{2,1,0:T(8,128)(2,1)} fusion(f32[64,288]{1,0:T(8,128)S(1)} %copy.23, bf16[64,288,128]{2,1,0:T(8,128)(2,1)} %bitcast.56), kind=kLoop, calls=%fused_computation.2 | loop fusion | flops 7077888 | bytes 9510912 | tf_op jit(solution)/shard_map/convert_element_type | solution.py:82
  23.8 19.1 %all-to-all-start = ((bf16[64,288,128]{2,1,0:T(8,128)(2,1)}), bf16[64,288,128]{2,1,0:T(8,128)(2,1)}, u32[]{:S(2)}, u32[]{:S(2)}) async-start(bf16[64,288,128]{2,1,0:T(8,128)(2,1)} %fusion), calls=%async_computation | async-start | bytes 9437184 | tf_op jit(solution)/shard_map/all_to_all | solution.py:40
  43.0 0.7 all-gather.4.cloned.1.call-update
  43.7 13.6 %all-gather = bf16[1,384,1024]{2,1,0:T(8,128)(2,1)S(1)} all-gather(bf16[1,48,1024]{2,1,0:T(8,128)(2,1)S(1)} %copy-done.4), channel_id=2, replica_groups=mesh['dp'=8,'expert'=64] {'dp'}, dimensions={1}, use_global_device_ids=true | all-gather | bytes 884736 | tf_op jit(solution)/shard_map/all_gather | solution.py:90
  57.2 196.4 %all-to-all-done = bf16[64,288,128]{2,1,0:T(8,128)(2,1)} async-done(((bf16[64,288,128]{2,1,0:T(8,128)(2,1)}), bf16[64,288,128]{2,1,0:T(8,128)(2,1)}, u32[]{:S(2)}, u32[]{:S(2)}) %all-to-all-start) | async-done | bytes 4718624 | tf_op jit(solution)/shard_map/all_to_all | solution.py:40
  253.6 3.6 fusion.44
  257.2 4.7 %fusion.7 = f32[1152,768]{0,1:T(8,128)S(1)} fusion(bf16[144,8,8,128]{3,2,1,0:T(8,128)(2,1)S(1)} %bitcast.59, bf16[1,1024,768]{2,1,0:T(8,128)(2,1)} %all-gather.4.cloned.1.call-done), kind=kOutput, calls=%fused_computation.14 | convolution fusion | flops 1811939328 | bytes 7471104 | tf_op jit(solution)/shard_map/dot_general | solution.py:92
  261.9 1.7 multiply_convert_fusion.2
  263.7 0.9 copy-done.7
  264.6 0.3 copy-done.8
  264.9 2.1 convolution_convert_fusion
  267.0 2.5 reshape_reshape.3
  269.4 7.2 %all-to-all-start.1 = ((bf16[64,144,128]{2,1,0:T(8,128)(2,1)}), bf16[64,144,128]{2,1,0:T(8,128)(2,1)S(1)}, u32[]{:S(2)}, u32[]{:S(2)}) async-start(bf16[64,144,128]{2,1,0:T(8,128)(2,1)} %reshape_reshape.3), calls=%async_computation.1 | async-start | bytes 4718592 | tf_op jit(solution)/shard_map/all_to_all | solution.py:40
  276.7 4.9 %fusion.23 = bf16[384,1024]{1,0:T(8,128)(2,1)} fusion(bf16[144,8,8,128]{3,2,1,0:T(8,128)(2,1)} %bitcast.61, f32[1152,768]{0,1:T(8,128)} %copy-done.6), kind=kOutput, calls=%fused_computation.33 | convolution fusion | flops 909017088 | bytes 6684672 | tf_op jit(solution)/shard_map/dot_general | solution.py:26
  281.6 0.3 reduce-scatter.3.cloned.1.call-start
  281.9 5.6 %fusion.18 = bf16[1024,768]{1,0:T(8,128)(2,1)} fusion(bf16[144,8,8,128]{3,2,1,0:T(8,128)(2,1)} %bitcast.60, bf16[1152,384]{0,1:T(8,128)(2,1)} %copy-done.8, bf16[1152,384]{0,1:T(8,128)(2,1)} %copy-done.7), kind=kOutput, calls=%fused_computation.30 | convolution fusion | flops 1816264704 | bytes 5701632 | tf_op jit(solution)/shard_map/dot_general | solution.py:26
  287.5 32.1 %reduce-scatter.5.cloned.1.call-done = bf16[48,1024]{1,0:T(8,128)(2,1)} async-done(((bf16[384,1024]{1,0:T(8,128)(2,1)}), bf16[48,1024]{1,0:T(8,128)(2,1)}) %reduce-scatter.5.cloned.1.call-update) | async-done | bytes 98320 | tf_op jit(solution)/shard_map/reduce_scatter | solution.py:105
  319.6 1.6 bitcast_convert_fusion.1
  321.1 41.4 %reduce-scatter.3.cloned.1.call-done = bf16[128,768]{1,0:T(8,128)(2,1)} async-done(((bf16[1024,768]{1,0:T(8,128)(2,1)}), bf16[128,768]{1,0:T(8,128)(2,1)}) %reduce-scatter.3.cloned.1.call-update) | async-done | bytes 196624 | tf_op jit(solution)/shard_map/reduce_scatter | solution.py:99
  362.6 1.7 bitcast_convert_fusion
  364.3 21.1 %all-to-all-done.1 = bf16[64,144,128]{2,1,0:T(8,128)(2,1)S(1)} async-done(((bf16[64,144,128]{2,1,0:T(8,128)(2,1)}), bf16[64,144,128]{2,1,0:T(8,128)(2,1)S(1)}, u32[]{:S(2)}, u32[]{:S(2)}) %all-to-all-start.1) | async-done | bytes 2359328 | tf_op jit(solution)/shard_map/all_to_all | solution.py:40
  385.3 2.8 copy.24
  388.1 4.2 %fusion.26 = f32[128,1024]{0,1:S(1)} fusion(bf16[1152,1024]{0,1:T(8,128)(2,1)} %bitcast.58, s32[1024]{0:T(1024)S(1)} %get-tuple-element.17, s32[1024]{0:T(1024)S(1)} %get-tuple-element.16), kind=kOutput, calls=%fused_computation.34 | convolution fusion | flops 605437952 | bytes 2891776
  392.4 0.9 copy.25
  (39 shorter events, 1.5 us)
Async XLA Ops:
  7.2 5.3 %copy-start.2 = (bf16[128,1024]{1,0:T(8,128)(2,1)S(1)}, bf16[128,1024]{1,0:T(8,128)(2,1)}, u32[]{:S(2)}) copy-start(bf16[128,1024]{1,0:T(8,128)(2,1)} %param.6) | copy-start | bytes 786436
  7.2 5.4 %copy-start.3 = (bf16[128,1024]{1,0:T(8,128)(2,1)S(1)}, bf16[128,1024]{1,0:T(8,128)(2,1)}, u32[]{:S(2)}) copy-start(bf16[128,1024]{1,0:T(8,128)(2,1)} %param.7) | copy-start | bytes 786436
  23.8 19.8 %copy-start.4 = (bf16[1,48,1024]{2,1,0:T(8,128)(2,1)S(1)}, bf16[1,48,1024]{2,1,0:T(8,128)(2,1)}, u32[]{:S(2)}) copy-start(bf16[1,48,1024]{2,1,0:T(8,128)(2,1)} %param.11) | copy-start | bytes 294916
  23.8 229.8 %all-to-all-start = ((bf16[64,288,128]{2,1,0:T(8,128)(2,1)}), bf16[64,288,128]{2,1,0:T(8,128)(2,1)}, u32[]{:S(2)}, u32[]{:S(2)}) async-start(bf16[64,288,128]{2,1,0:T(8,128)(2,1)} %fusion), calls=%async_computation | async-start | bytes 9437184 | tf_op jit(solution)/shard_map/all_to_all | solution.py:40
  42.9 214.3 %all-gather.4.cloned.1.call-start = ((), (), s32[]{:S(2)}) async-start(), calls=%async_computation.6 | async-start | bytes 1769472 | tf_op jit(solution)/shard_map/all_gather | solution.py:89
  257.2 4.7 %copy-start = (bf16[1152,8,128]{2,1,0:T(8,128)(2,1)}, bf16[1152,8,128]{2,1,0:T(8,128)(2,1)S(1)}, u32[]{:S(2)}) copy-start(bf16[1152,8,128]{2,1,0:T(8,128)(2,1)S(1)} %get-tuple-element.14) | copy-start | bytes 7077892
  257.2 4.7 %copy-start.1 = (bf16[1152,8,128]{2,1,0:T(8,128)(2,1)S(1)}, bf16[1152,8,128]{2,1,0:T(8,128)(2,1)}, u32[]{:S(2)}) copy-start(bf16[1152,8,128]{2,1,0:T(8,128)(2,1)} %get-tuple-element.15) | copy-start | bytes 7077892
  261.9 1.8 copy-start.6
  261.9 3.0 copy-start.5
  263.7 0.9 copy-start.7
  263.7 1.2 copy-start.8
  269.4 115.9 %all-to-all-start.1 = ((bf16[64,144,128]{2,1,0:T(8,128)(2,1)}), bf16[64,144,128]{2,1,0:T(8,128)(2,1)S(1)}, u32[]{:S(2)}, u32[]{:S(2)}) async-start(bf16[64,144,128]{2,1,0:T(8,128)(2,1)} %reshape_reshape.3), calls=%async_computation.1 | async-start | bytes 4718592 | tf_op jit(solution)/shard_map/all_to_all | solution.py:40
  276.6 42.9 %reduce-scatter.5.cloned.1.call-start = ((), (), s32[]{:S(2)}) async-start(), calls=%async_computation.5 | async-start | bytes 884736 | tf_op jit(solution)/shard_map/reduce_scatter | solution.py:105
  281.6 80.9 %reduce-scatter.3.cloned.1.call-start = ((), (), s32[]{:S(2)}) async-start(), calls=%async_computation.4 | async-start | bytes 1769472 | tf_op jit(solution)/shard_map/reduce_scatter | solution.py:99
Sparse Core Ops, SparseCore 0:
  45.8 31.0 all-gather.3
  281.8 37.7 reduce-scatter.4
  322.4 40.0 reduce-scatter.2

commit v6 on v5

--- a/solution.py
+++ b/solution.py
@@ -69,17 +69,19 @@
         slot_hits.astype(jnp.bfloat16), token_of_route, preferred_element_type=jnp.float32
     ).astype(jnp.bfloat16)
     chunks = model_width // 128
-    both_rows = jnp.concatenate(
-        [tokens.reshape(token_rows, chunks, 128), grad_out.reshape(token_rows, chunks, 128)],
-        axis=1,
+    token_parts = tokens.reshape(token_rows, 1, chunks, 128)
+    grad_parts = grad_out.reshape(token_rows, 1, chunks, 128).astype(jnp.float32)
+    route_tokens = jnp.broadcast_to(token_parts, (token_rows, route_width, chunks, 128))
+    route_grads = (gates[:, :, None, None] * grad_parts).astype(jnp.bfloat16)
+    route_rows = jnp.concatenate([route_tokens, route_grads], axis=2).reshape(
+        route_total, 2 * chunks, 128
+    )
+    route_rows = jnp.concatenate(
+        [route_rows, jnp.zeros((1, 2 * chunks, 128), jnp.bfloat16)], axis=0
     )
     slot_routes = jnp.sum(jnp.where(slot_hits, route_index[None, :], 0), axis=1)
     occupied = jnp.any(slot_hits, axis=1)
-    picked = both_rows[slot_routes // route_width].astype(jnp.float32)
-    chunk_index = jnp.arange(2 * chunks, dtype=jnp.int32)[None, :, None]
-    row_scale = jnp.where(chunk_index < chunks, jnp.ones((), jnp.float32), slot_gates[:, None, None])
-    row_scale = jnp.where(occupied[:, None, None], row_scale, jnp.zeros((), jnp.float32))
-    send_both = (row_scale * picked).astype(jnp.bfloat16)
+    send_both = route_rows[jnp.where(occupied, slot_routes, route_total)]
     recv_both = expert_exchange(send_both, expert_count)
     slot_tokens = recv_both[:, :chunks, :].reshape(slot_total, model_width)
     slot_grads = recv_both[:, chunks:, :].reshape(slot_total, model_width)

time: 400 us -> 403 us (level)
  no operation moved by 1% of the time
where the time goes in v6:
time: 403 us; the launch traced here: 402 us
  waiting for transfers between devices  292 us (72%)
  starting transfers between devices  26.6 us (7%)
  matrix products  23.7 us (6%)
  local copies, waits for them, and re-layouts  21.5 us (5%)
  between operations  14 us (3%)
  blocking collectives  13.6 us (3%)
  other arithmetic  11.1 us (3%)
    all_to_all x2, waiting for transfers between devices, expert_exchange(): blocks = lax.all_to_all(blocks, 'expert', 0, 0, tiled=True)  217 us
    reduce_scatter x1, waiting for transfers between devices, on_device(): lax.psum_scatter(contract_first(slot_tokens, pre_grad).astype(jnp.bfloat1...  41.4 us
    reduce_scatter x1, waiting for transfers between devices, on_device(): lax.psum_scatter(contract_first(hidden_act, slot_grads).astype(jnp.bfloat...  32 us
    all_to_all x2, starting transfers between devices, expert_exchange(): blocks = lax.all_to_all(blocks, 'expert', 0, 0, tiled=True)  26.3 us
    all_gather x1, blocking collectives, on_device(): lax.all_gather(local_down, 'dp', axis=0, tiled=True)  13.6 us
    dot_general x2, matrix products, contract_first(): lax.dot_general(left, right, (((0,), (0,)), ((), ())), preferred_element_...  10.5 us
    gather x1, local copies, waits for them, and re-layouts, on_device(): send_both = route_rows[jnp.where(occupied, slot_routes, route_total)]  8.19 us
  transfers between devices with their start and end apart: 5, of which 4 were waited for; matrix products, arithmetic and copies ran while one was open for 4% of the time, Pallas kernels for 0%

profile of v6, /device:TPU:6, one launch (start us, length us, event | category | flops | bytes accessed | tf_op | source)
XLA Modules:
  0.0 402.0 jit_solution(10409720929908116071)
XLA Ops:
  7.2 0.8 copy.14
  8.1 0.6 fusion.33
  8.7 0.6 fusion.2
  9.4 0.6 select_reduce_fusion
  10.0 0.8 copy.15
  11.1 2.9 fusion.5
  13.9 0.3 broadcast_in_dim.47
  14.2 3.6 fusion.4
  17.8 8.2 %gather_fusion = bf16[1152,16,128]{2,1,0:T(8,128)(2,1)} fusion(bf16[1025,16,128]{2,1,0:T(8,128)(2,1)} %fusion.4, s32[2048]{0:T(1024)S(1)} %pad_clamp_fusion), kind=kCustom, calls=%fused_computation | custom fusion | bytes 9441792 | tf_op jit(solution)/shard_map/gather | solution.py:84
  26.0 19.1 %all-to-all-start = ((bf16[64,288,128]{2,1,0:T(8,128)(2,1)}), bf16[64,288,128]{2,1,0:T(8,128)(2,1)}, u32[]{:S(2)}, u32[]{:S(2)}) async-start(bf16[64,288,128]{2,1,0:T(8,128)(2,1)} %bitcast.51), calls=%async_computation | async-start | bytes 9437184 | tf_op jit(solution)/shard_map/all_to_all | solution.py:40
  45.2 0.7 all-gather.4.cloned.1.call-update
  45.9 13.6 %all-gather = bf16[1,384,1024]{2,1,0:T(8,128)(2,1)S(1)} all-gather(bf16[1,48,1024]{2,1,0:T(8,128)(2,1)S(1)} %copy-done.4), channel_id=2, replica_groups=mesh['dp'=8,'expert'=64] {'dp'}, dimensions={1}, use_global_device_ids=true | all-gather | bytes 884736 | tf_op jit(solution)/shard_map/all_gather | solution.py:92
  59.4 196.4 %all-to-all-done = bf16[64,288,128]{2,1,0:T(8,128)(2,1)} async-done(((bf16[64,288,128]{2,1,0:T(8,128)(2,1)}), bf16[64,288,128]{2,1,0:T(8,128)(2,1)}, u32[]{:S(2)}, u32[]{:S(2)}) %all-to-all-start) | async-done | bytes 4718624 | tf_op jit(solution)/shard_map/all_to_all | solution.py:40
  255.8 3.6 fusion.46
  259.4 4.7 %fusion.10 = f32[1152,768]{0,1:T(8,128)S(1)} fusion(bf16[144,8,8,128]{3,2,1,0:T(8,128)(2,1)S(1)} %bitcast.55, bf16[1,1024,768]{2,1,0:T(8,128)(2,1)} %all-gather.4.cloned.1.call-done), kind=kOutput, calls=%fused_computation.17 | convolution fusion | flops 1811939328 | bytes 7471104 | tf_op jit(solution)/shard_map/dot_general | solution.py:94
  264.1 1.7 multiply_convert_fusion.2
  265.9 0.9 copy-done.7
  266.9 0.3 copy-done.8
  267.2 2.1 convolution_convert_fusion
  269.2 2.4 reshape_reshape.3
  271.7 7.2 %all-to-all-start.1 = ((bf16[64,144,128]{2,1,0:T(8,128)(2,1)}), bf16[64,144,128]{2,1,0:T(8,128)(2,1)S(1)}, u32[]{:S(2)}, u32[]{:S(2)}) async-start(bf16[64,144,128]{2,1,0:T(8,128)(2,1)} %reshape_reshape.3), calls=%async_computation.1 | async-start | bytes 4718592 | tf_op jit(solution)/shard_map/all_to_all | solution.py:40
  278.9 4.9 %fusion.26 = bf16[384,1024]{1,0:T(8,128)(2,1)} fusion(bf16[144,8,8,128]{3,2,1,0:T(8,128)(2,1)} %bitcast.57, f32[1152,768]{0,1:T(8,128)} %copy-done.6), kind=kOutput, calls=%fused_computation.36 | convolution fusion | flops 909017088 | bytes 6684672 | tf_op jit(solution)/shard_map/dot_general | solution.py:26
  283.8 0.3 reduce-scatter.3.cloned.1.call-start
  284.1 5.6 %fusion.21 = bf16[1024,768]{1,0:T(8,128)(2,1)} fusion(bf16[144,8,8,128]{3,2,1,0:T(8,128)(2,1)} %bitcast.56, bf16[1152,384]{0,1:T(8,128)(2,1)} %copy-done.8, bf16[1152,384]{0,1:T(8,128)(2,1)} %copy-done.7), kind=kOutput, calls=%fused_computation.33 | convolution fusion | flops 1816264704 | bytes 5701632 | tf_op jit(solution)/shard_map/dot_general | solution.py:26
  289.7 32.0 %reduce-scatter.5.cloned.1.call-done = bf16[48,1024]{1,0:T(8,128)(2,1)} async-done(((bf16[384,1024]{1,0:T(8,128)(2,1)}), bf16[48,1024]{1,0:T(8,128)(2,1)}) %reduce-scatter.5.cloned.1.call-update) | async-done | bytes 98320 | tf_op jit(solution)/shard_map/reduce_scatter | solution.py:107
  321.7 1.6 bitcast_convert_fusion.1
  323.3 41.4 %reduce-scatter.3.cloned.1.call-done = bf16[128,768]{1,0:T(8,128)(2,1)} async-done(((bf16[1024,768]{1,0:T(8,128)(2,1)}), bf16[128,768]{1,0:T(8,128)(2,1)}) %reduce-scatter.3.cloned.1.call-update) | async-done | bytes 196624 | tf_op jit(solution)/shard_map/reduce_scatter | solution.py:101
  364.7 1.7 bitcast_convert_fusion
  366.4 21.1 %all-to-all-done.1 = bf16[64,144,128]{2,1,0:T(8,128)(2,1)S(1)} async-done(((bf16[64,144,128]{2,1,0:T(8,128)(2,1)}), bf16[64,144,128]{2,1,0:T(8,128)(2,1)S(1)}, u32[]{:S(2)}, u32[]{:S(2)}) %all-to-all-start.1) | async-done | bytes 2359328 | tf_op jit(solution)/shard_map/all_to_all | solution.py:40
  387.5 2.8 copy.16
  390.3 4.2 %fusion.29 = f32[128,1024]{0,1:S(1)} fusion(bf16[1152,1024]{0,1:T(8,128)(2,1)} %bitcast.54, s32[1024]{0:T(1024)S(1)} %get-tuple-element.17, s32[1024]{0:T(1024)S(1)} %get-tuple-element.16), kind=kOutput, calls=%fused_computation.37 | convolution fusion | flops 605437952 | bytes 2891776
  394.6 0.8 copy.17
  (31 shorter events, 0.7 us)
Async XLA Ops:
  7.2 3.7 copy-start.3
  7.2 3.7 copy-start.2
  26.0 19.8 %copy-start.4 = (bf16[1,48,1024]{2,1,0:T(8,128)(2,1)S(1)}, bf16[1,48,1024]{2,1,0:T(8,128)(2,1)}, u32[]{:S(2)}) copy-start(bf16[1,48,1024]{2,1,0:T(8,128)(2,1)} %param.11) | copy-start | bytes 294916
  26.0 229.8 %all-to-all-start = ((bf16[64,288,128]{2,1,0:T(8,128)(2,1)}), bf16[64,288,128]{2,1,0:T(8,128)(2,1)}, u32[]{:S(2)}, u32[]{:S(2)}) async-start(bf16[64,288,128]{2,1,0:T(8,128)(2,1)} %bitcast.51), calls=%async_computation | async-start | bytes 9437184 | tf_op jit(solution)/shard_map/all_to_all | solution.py:40
  45.1 214.3 %all-gather.4.cloned.1.call-start = ((), (), s32[]{:S(2)}) async-start(), calls=%async_computation.6 | async-start | bytes 1769472 | tf_op jit(solution)/shard_map/all_gather | solution.py:91
  259.4 4.7 %copy-start = (bf16[1152,8,128]{2,1,0:T(8,128)(2,1)}, bf16[1152,8,128]{2,1,0:T(8,128)(2,1)S(1)}, u32[]{:S(2)}) copy-start(bf16[1152,8,128]{2,1,0:T(8,128)(2,1)S(1)} %get-tuple-element.14) | copy-start | bytes 7077892
  259.4 4.7 %copy-start.1 = (bf16[1152,8,128]{2,1,0:T(8,128)(2,1)S(1)}, bf16[1152,8,128]{2,1,0:T(8,128)(2,1)}, u32[]{:S(2)}) copy-start(bf16[1152,8,128]{2,1,0:T(8,128)(2,1)} %get-tuple-element.15) | copy-start | bytes 7077892
  264.1 1.8 copy-start.6
  264.1 3.0 copy-start.5
  265.9 0.9 copy-start.7
  265.9 1.2 copy-start.8
  271.7 115.9 %all-to-all-start.1 = ((bf16[64,144,128]{2,1,0:T(8,128)(2,1)}), bf16[64,144,128]{2,1,0:T(8,128)(2,1)S(1)}, u32[]{:S(2)}, u32[]{:S(2)}) async-start(bf16[64,144,128]{2,1,0:T(8,128)(2,1)} %reshape_reshape.3), calls=%async_computation.1 | async-start | bytes 4718592 | tf_op jit(solution)/shard_map/all_to_all | solution.py:40
  278.8 42.9 %reduce-scatter.5.cloned.1.call-start = ((), (), s32[]{:S(2)}) async-start(), calls=%async_computation.5 | async-start | bytes 884736 | tf_op jit(solution)/shard_map/reduce_scatter | solution.py:107
  283.8 80.9 %reduce-scatter.3.cloned.1.call-start = ((), (), s32[]{:S(2)}) async-start(), calls=%async_computation.4 | async-start | bytes 1769472 | tf_op jit(solution)/shard_map/reduce_scatter | solution.py:101
Sparse Core Ops, SparseCore 0:
  48.1 31.0 all-gather.3
  283.9 37.7 reduce-scatter.4
  324.6 40.1 reduce-scatter.2

commit v7 on v5

--- a/solution.py
+++ b/solution.py
@@ -109,8 +109,9 @@
         tiled=True,
     ).astype(jnp.float32)
     slot_return = expert_exchange(slot_back, expert_count)
+    per_route = slot_return[targets].astype(jnp.float32)
     grad_tokens = (
-        contract_first(slot_of_token, slot_return)
+        jnp.sum(per_route.reshape(token_rows, route_width, chunks, 128), axis=1)
         .astype(jnp.bfloat16)
         .reshape(token_rows, model_width)
     )

time: 400 us -> 403 us (level)
  local copies, waits for them, and re-layouts: 18.8 us -> 23.6 us
  matrix products: 23.7 us -> 19.5 us
    gather x0 -> x1, local copies, waits for them, and re-layouts: none -> 7.54 us  [on_device(): per_route = slot_return[targets].astype(jnp.float32)]
    unnamed x1 -> x0, matrix products: 4.19 us -> none
where the time goes in v7:
time: 403 us; the launch traced here: 402 us
  waiting for transfers between devices  292 us (72%)
  starting transfers between devices  26.4 us (7%)
  local copies, waits for them, and re-layouts  23.6 us (6%)
  matrix products  19.5 us (5%)
  between operations  14 us (3%)
  other arithmetic  13.6 us (3%)
  blocking collectives  13.6 us (3%)
    all_to_all x2, waiting for transfers between devices, expert_exchange(): blocks = lax.all_to_all(blocks, 'expert', 0, 0, tiled=True)  217 us
    reduce_scatter x1, waiting for transfers between devices, on_device(): lax.psum_scatter(contract_first(slot_tokens, pre_grad).astype(jnp.bfloat1...  41.4 us
    reduce_scatter x1, waiting for transfers between devices, on_device(): lax.psum_scatter(contract_first(hidden_act, slot_grads).astype(jnp.bfloat...  32 us
    all_to_all x2, starting transfers between devices, expert_exchange(): blocks = lax.all_to_all(blocks, 'expert', 0, 0, tiled=True)  26.3 us
    all_gather x1, blocking collectives, on_device(): lax.all_gather(local_down, 'dp', axis=0, tiled=True)  13.6 us
    dot_general x2, matrix products, contract_first(): lax.dot_general(left, right, (((0,), (0,)), ((), ())), preferred_element_...  10.5 us
  transfers between devices with their start and end apart: 5, of which 4 were waited for; matrix products, arithmetic and copies ran while one was open for 4% of the time, Pallas kernels for 0%

profile of v7, /device:TPU:6, one launch (start us, length us, event | category | flops | bytes accessed | tf_op | source)
XLA Modules:
  0.0 402.3 jit_solution(12113397395340218235)
XLA Ops:
  7.2 0.8 copy.16
  8.1 0.6 fusion.26
  8.7 0.6 fusion.1
  9.4 0.6 select_reduce_fusion
  9.9 0.8 copy.18
  10.8 0.6 select_reduce_fusion.1
  11.6 0.2 broadcast_in_dim.91
  11.9 0.3 broadcast_in_dim.95
  12.7 4.8 %gather_fusion = bf16[1152,16,128]{2,1,0:T(8,128)(2,1)} fusion(bf16[128,16,128]{2,1,0:T(8,128)(2,1)S(1)} %pad_maximum_fusion.3, s32[2048]{0:T(1024)S(1)} %pad_clamp_fusion), kind=kCustom, calls=%fused_computation | custom fusion | bytes 9441792 | tf_op jit(solution)/shard_map/gather | solution.py:78
  17.5 6.3 %fusion = bf16[64,288,128]{2,1,0:T(8,128)(2,1)} fusion(f32[64,288]{1,0:T(8,128)S(1)} %copy.21, bf16[64,288,128]{2,1,0:T(8,128)(2,1)} %bitcast.60), kind=kLoop, calls=%fused_computation.3 | loop fusion | flops 7077888 | bytes 9510912 | tf_op jit(solution)/shard_map/convert_element_type | solution.py:82
  23.8 19.1 %all-to-all-start = ((bf16[64,288,128]{2,1,0:T(8,128)(2,1)}), bf16[64,288,128]{2,1,0:T(8,128)(2,1)}, u32[]{:S(2)}, u32[]{:S(2)}) async-start(bf16[64,288,128]{2,1,0:T(8,128)(2,1)} %fusion), calls=%async_computation | async-start | bytes 9437184 | tf_op jit(solution)/shard_map/all_to_all | solution.py:40
  43.0 0.7 all-gather.4.cloned.1.call-update
  43.7 13.6 %all-gather = bf16[1,384,1024]{2,1,0:T(8,128)(2,1)S(1)} all-gather(bf16[1,48,1024]{2,1,0:T(8,128)(2,1)S(1)} %copy-done.4), channel_id=2, replica_groups=mesh['dp'=8,'expert'=64] {'dp'}, dimensions={1}, use_global_device_ids=true | all-gather | bytes 884736 | tf_op jit(solution)/shard_map/all_gather | solution.py:90
  57.2 196.4 %all-to-all-done = bf16[64,288,128]{2,1,0:T(8,128)(2,1)} async-done(((bf16[64,288,128]{2,1,0:T(8,128)(2,1)}), bf16[64,288,128]{2,1,0:T(8,128)(2,1)}, u32[]{:S(2)}, u32[]{:S(2)}) %all-to-all-start) | async-done | bytes 4718624 | tf_op jit(solution)/shard_map/all_to_all | solution.py:40
  253.6 3.6 fusion.35
  257.2 4.7 %fusion.5 = f32[1152,768]{0,1:T(8,128)S(1)} fusion(bf16[144,8,8,128]{3,2,1,0:T(8,128)(2,1)S(1)} %bitcast.62, bf16[1,1024,768]{2,1,0:T(8,128)(2,1)} %all-gather.4.cloned.1.call-done), kind=kOutput, calls=%fused_computation.13 | convolution fusion | flops 1811939328 | bytes 7471104 | tf_op jit(solution)/shard_map/dot_general | solution.py:92
  261.9 1.7 multiply_convert_fusion.2
  263.7 0.9 copy-done.8
  264.6 0.3 copy-done.9
  264.9 2.1 convolution_convert_fusion
  267.0 2.4 reshape_reshape.3
  269.4 7.2 %all-to-all-start.1 = ((bf16[64,144,128]{2,1,0:T(8,128)(2,1)}), bf16[64,144,128]{2,1,0:T(8,128)(2,1)S(1)}, u32[]{:S(2)}, u32[]{:S(2)}) async-start(bf16[64,144,128]{2,1,0:T(8,128)(2,1)} %reshape_reshape.3), calls=%async_computation.1 | async-start | bytes 4718592 | tf_op jit(solution)/shard_map/all_to_all | solution.py:40
  276.6 5.0 %fusion.20 = bf16[384,1024]{1,0:T(8,128)(2,1)} fusion(bf16[144,8,8,128]{3,2,1,0:T(8,128)(2,1)} %bitcast.64, f32[1152,768]{0,1:T(8,128)} %copy-done.7), kind=kOutput, calls=%fused_computation.32 | convolution fusion | flops 909017088 | bytes 6684672 | tf_op jit(solution)/shard_map/dot_general | solution.py:26
  281.7 5.5 %fusion.15 = bf16[1024,768]{1,0:T(8,128)(2,1)} fusion(bf16[144,8,8,128]{3,2,1,0:T(8,128)(2,1)} %bitcast.63, bf16[1152,384]{0,1:T(8,128)(2,1)} %copy-done.9, bf16[1152,384]{0,1:T(8,128)(2,1)} %copy-done.8), kind=kOutput, calls=%fused_computation.29 | convolution fusion | flops 1816264704 | bytes 5701632 | tf_op jit(solution)/shard_map/dot_general | solution.py:26
  287.5 32.0 %reduce-scatter.5.cloned.1.call-done = bf16[48,1024]{1,0:T(8,128)(2,1)} async-done(((bf16[384,1024]{1,0:T(8,128)(2,1)}), bf16[48,1024]{1,0:T(8,128)(2,1)}) %reduce-scatter.5.cloned.1.call-update) | async-done | bytes 98320 | tf_op jit(solution)/shard_map/reduce_scatter | solution.py:105
  319.5 1.6 bitcast_convert_fusion.1
  321.1 41.4 %reduce-scatter.3.cloned.1.call-done = bf16[128,768]{1,0:T(8,128)(2,1)} async-done(((bf16[1024,768]{1,0:T(8,128)(2,1)}), bf16[128,768]{1,0:T(8,128)(2,1)}) %reduce-scatter.3.cloned.1.call-update) | async-done | bytes 196624 | tf_op jit(solution)/shard_map/reduce_scatter | solution.py:99
  362.5 1.7 bitcast_convert_fusion
  364.2 21.1 %all-to-all-done.1 = bf16[64,144,128]{2,1,0:T(8,128)(2,1)S(1)} async-done(((bf16[64,144,128]{2,1,0:T(8,128)(2,1)}), bf16[64,144,128]{2,1,0:T(8,128)(2,1)S(1)}, u32[]{:S(2)}, u32[]{:S(2)}) %all-to-all-start.1) | async-done | bytes 2359328 | tf_op jit(solution)/shard_map/all_to_all | solution.py:40
  385.3 7.5 %gather_fusion.1 = bf16[1024,8,128]{2,1,0:T(8,128)(2,1)} fusion(bf16[1152,8,128]{2,1,0:T(8,128)(2,1)S(1)} %bitcast.61, s32[1024]{0:T(1024)S(1)} %broadcast_clamp_fusion), kind=kCustom, calls=%fused_computation.1 | custom fusion | bytes 4198400 | tf_op jit(solution)/shard_map/gather | solution.py:112
  392.9 2.1 bitcast_reduce_fusion
  395.0 0.8 copy.51
  (45 shorter events, 1.6 us)
Async XLA Ops:
  7.2 5.3 %copy-start.2 = (bf16[128,1024]{1,0:T(8,128)(2,1)S(1)}, bf16[128,1024]{1,0:T(8,128)(2,1)}, u32[]{:S(2)}) copy-start(bf16[128,1024]{1,0:T(8,128)(2,1)} %param.6) | copy-start | bytes 786436
  7.2 5.4 %copy-start.3 = (bf16[128,1024]{1,0:T(8,128)(2,1)S(1)}, bf16[128,1024]{1,0:T(8,128)(2,1)}, u32[]{:S(2)}) copy-start(bf16[128,1024]{1,0:T(8,128)(2,1)} %param.7) | copy-start | bytes 786436
  23.8 19.8 %copy-start.4 = (bf16[1,48,1024]{2,1,0:T(8,128)(2,1)S(1)}, bf16[1,48,1024]{2,1,0:T(8,128)(2,1)}, u32[]{:S(2)}) copy-start(bf16[1,48,1024]{2,1,0:T(8,128)(2,1)} %param.11) | copy-start | bytes 294916
  23.8 229.8 %all-to-all-start = ((bf16[64,288,128]{2,1,0:T(8,128)(2,1)}), bf16[64,288,128]{2,1,0:T(8,128)(2,1)}, u32[]{:S(2)}, u32[]{:S(2)}) async-start(bf16[64,288,128]{2,1,0:T(8,128)(2,1)} %fusion), calls=%async_computation | async-start | bytes 9437184 | tf_op jit(solution)/shard_map/all_to_all | solution.py:40
  42.9 214.3 %all-gather.4.cloned.1.call-start = ((), (), s32[]{:S(2)}) async-start(), calls=%async_computation.6 | async-start | bytes 1769472 | tf_op jit(solution)/shard_map/all_gather | solution.py:89
  257.2 4.7 %copy-start = (bf16[1152,8,128]{2,1,0:T(8,128)(2,1)}, bf16[1152,8,128]{2,1,0:T(8,128)(2,1)S(1)}, u32[]{:S(2)}) copy-start(bf16[1152,8,128]{2,1,0:T(8,128)(2,1)S(1)} %get-tuple-element.5) | copy-start | bytes 7077892
  257.2 4.7 %copy-start.1 = (bf16[1152,8,128]{2,1,0:T(8,128)(2,1)S(1)}, bf16[1152,8,128]{2,1,0:T(8,128)(2,1)}, u32[]{:S(2)}) copy-start(bf16[1152,8,128]{2,1,0:T(8,128)(2,1)} %get-tuple-element.6) | copy-start | bytes 7077892
  261.9 1.8 copy-start.7
  261.9 3.0 copy-start.6
  263.7 0.9 copy-start.8
  263.7 1.2 copy-start.9
  269.4 115.9 %all-to-all-start.1 = ((bf16[64,144,128]{2,1,0:T(8,128)(2,1)}), bf16[64,144,128]{2,1,0:T(8,128)(2,1)S(1)}, u32[]{:S(2)}, u32[]{:S(2)}) async-start(bf16[64,144,128]{2,1,0:T(8,128)(2,1)} %reshape_reshape.3), calls=%async_computation.1 | async-start | bytes 4718592 | tf_op jit(solution)/shard_map/all_to_all | solution.py:40
  276.6 43.0 %reduce-scatter.5.cloned.1.call-start = ((), (), s32[]{:S(2)}) async-start(), calls=%async_computation.5 | async-start | bytes 884736 | tf_op jit(solution)/shard_map/reduce_scatter | solution.py:105
  281.6 5.6 %copy-start.5 = (s32[128,8]{0,1:T(8,128)S(1)}, s32[128,8]{0,1:T(8,128)}, u32[]{:S(2)}) copy-start(s32[128,8]{0,1:T(8,128)} %param.8) | copy-start | bytes 12292
  281.6 80.9 %reduce-scatter.3.cloned.1.call-start = ((), (), s32[]{:S(2)}) async-start(), calls=%async_computation.4 | async-start | bytes 1769472 | tf_op jit(solution)/shard_map/reduce_scatter | solution.py:99
Sparse Core Ops, SparseCore 0:
  45.8 31.0 all-gather.3
  281.7 37.7 reduce-scatter.4
  322.4 40.1 reduce-scatter.2

commit v8 on v5

--- a/solution.py
+++ b/solution.py
@@ -75,11 +75,11 @@
     )
     slot_routes = jnp.sum(jnp.where(slot_hits, route_index[None, :], 0), axis=1)
     occupied = jnp.any(slot_hits, axis=1)
-    picked = both_rows[slot_routes // route_width].astype(jnp.float32)
-    chunk_index = jnp.arange(2 * chunks, dtype=jnp.int32)[None, :, None]
-    row_scale = jnp.where(chunk_index < chunks, jnp.ones((), jnp.float32), slot_gates[:, None, None])
-    row_scale = jnp.where(occupied[:, None, None], row_scale, jnp.zeros((), jnp.float32))
-    send_both = (row_scale * picked).astype(jnp.bfloat16)
+    picked = both_rows[slot_routes // route_width]
+    picked_grads = picked[:, chunks:, :].astype(jnp.float32)
+    send_grads = (slot_gates[:, None, None] * picked_grads).astype(jnp.bfloat16)
+    send_tokens = jnp.where(occupied[:, None, None], picked[:, :chunks, :], jnp.zeros((), jnp.bfloat16))
+    send_both = jnp.concatenate([send_tokens, send_grads], axis=1)
     recv_both = expert_exchange(send_both, expert_count)
     slot_tokens = recv_both[:, :chunks, :].reshape(slot_total, model_width)
     slot_grads = recv_both[:, chunks:, :].reshape(slot_total, model_width)

time: 400 us -> 405 us (1.012)
  other arithmetic: 11.5 us -> 16.7 us
    select_n x2, other arithmetic: 0.08 us -> 4.29 us  [the longest x1 4.25 us: on_device(): jnp.where(occupied[:, None, None], picked[:, :chunks, :], jnp.zeros((), j...]
where the time goes in v8:
time: 405 us; the launch traced here: 404 us
  waiting for transfers between devices  292 us (72%)
  starting transfers between devices  26.6 us (7%)
  matrix products  23.6 us (6%)
  local copies, waits for them, and re-layouts  17.8 us (4%)
  other arithmetic  16.7 us (4%)
  between operations  14 us (3%)
  blocking collectives  13.6 us (3%)
    all_to_all x2, waiting for transfers between devices, expert_exchange(): blocks = lax.all_to_all(blocks, 'expert', 0, 0, tiled=True)  217 us
    reduce_scatter x1, waiting for transfers between devices, on_device(): lax.psum_scatter(contract_first(slot_tokens, pre_grad).astype(jnp.bfloat1...  41.5 us
    reduce_scatter x1, waiting for transfers between devices, on_device(): lax.psum_scatter(contract_first(hidden_act, slot_grads).astype(jnp.bfloat...  32.1 us
    all_to_all x2, starting transfers between devices, expert_exchange(): blocks = lax.all_to_all(blocks, 'expert', 0, 0, tiled=True)  26.3 us
    all_gather x1, blocking collectives, on_device(): lax.all_gather(local_down, 'dp', axis=0, tiled=True)  13.6 us
    dot_general x2, matrix products, contract_first(): lax.dot_general(left, right, (((0,), (0,)), ((), ())), preferred_element_...  10.5 us
  transfers between devices with their start and end apart: 5, of which 4 were waited for; matrix products, arithmetic and copies ran while one was open for 4% of the time, Pallas kernels for 0%

profile of v8, /device:TPU:6, one launch (start us, length us, event | category | flops | bytes accessed | tf_op | source)
XLA Modules:
  0.0 403.9 jit_solution(17370695066331995733)
XLA Ops:
  7.2 0.8 copy.14
  8.1 0.6 fusion.29
  8.7 0.6 fusion
  9.4 0.6 select_reduce_fusion.1
  10.0 0.8 copy.15
  10.8 0.6 select_reduce_fusion
  11.6 4.8 %gather_fusion = bf16[1152,16,128]{2,1,0:T(8,128)(2,1)} fusion(bf16[128,16,128]{2,1,0:T(8,128)(2,1)S(1)} %pad_maximum_fusion.4, s32[2048]{0:T(1024)S(1)} %pad_clamp_fusion), kind=kCustom, calls=%fused_computation | custom fusion | bytes 9441792 | tf_op jit(solution)/shard_map/gather | solution.py:78
  16.5 4.6 %multiply_convert_fusion = bf16[1152,8,128]{2,1,0:T(8,128)(2,1)S(1)} fusion(bf16[1152,16,128]{2,1,0:T(8,128)(2,1)} %gather_fusion, f32[1152]{0:T(1024)S(1)} %select_reduce_fusion), kind=kLoop, calls=%fused_computation.2 | loop fusion | flops 3538944 | bytes 4723200 | tf_op jit(solution)/shard_map/convert_element_type | solution.py:80
  21.0 4.2 %slice_select_fusion = bf16[1152,8,128]{2,1,0:T(8,128)(2,1)S(1)} fusion(bf16[1152,16,128]{2,1,0:T(8,128)(2,1)S(1)} %copy-done, pred[1152]{0:T(1024)(128)(4,1)S(1)} %fusion), kind=kLoop, calls=%fused_computation.20 | loop fusion | flops 1179648 | bytes 4719744 | tf_op jit(solution)/shard_map/jit(_where)/select_n | solution.py:81
  25.3 2.7 pad_maximum_fusion
  27.9 19.1 %all-to-all-start = ((bf16[64,288,128]{2,1,0:T(8,128)(2,1)}), bf16[64,288,128]{2,1,0:T(8,128)(2,1)}, u32[]{:S(2)}, u32[]{:S(2)}) async-start(bf16[64,288,128]{2,1,0:T(8,128)(2,1)} %bitcast.45), calls=%async_computation | async-start | bytes 9437184 | tf_op jit(solution)/shard_map/all_to_all | solution.py:40
  47.1 0.7 all-gather.4.cloned.1.call-update
  47.8 13.6 %all-gather = bf16[1,384,1024]{2,1,0:T(8,128)(2,1)S(1)} all-gather(bf16[1,48,1024]{2,1,0:T(8,128)(2,1)S(1)} %copy-done.5), channel_id=2, replica_groups=mesh['dp'=8,'expert'=64] {'dp'}, dimensions={1}, use_global_device_ids=true | all-gather | bytes 884736 | tf_op jit(solution)/shard_map/all_gather | solution.py:90
  61.4 196.4 %all-to-all-done = bf16[64,288,128]{2,1,0:T(8,128)(2,1)} async-done(((bf16[64,288,128]{2,1,0:T(8,128)(2,1)}), bf16[64,288,128]{2,1,0:T(8,128)(2,1)}, u32[]{:S(2)}, u32[]{:S(2)}) %all-to-all-start) | async-done | bytes 4718624 | tf_op jit(solution)/shard_map/all_to_all | solution.py:40
  257.7 3.6 fusion.42
  261.3 4.7 %fusion.6 = f32[1152,768]{0,1:T(8,128)S(1)} fusion(bf16[144,8,8,128]{3,2,1,0:T(8,128)(2,1)S(1)} %bitcast.48, bf16[1,1024,768]{2,1,0:T(8,128)(2,1)} %all-gather.4.cloned.1.call-done), kind=kOutput, calls=%fused_computation.14 | convolution fusion | flops 1811939328 | bytes 7471104 | tf_op jit(solution)/shard_map/dot_general | solution.py:92
  266.1 1.7 multiply_convert_fusion.3
  267.8 0.9 copy-done.8
  268.8 0.3 copy-done.9
  269.1 2.1 convolution_convert_fusion
  271.1 2.4 reshape_reshape.3
  273.6 7.2 %all-to-all-start.1 = ((bf16[64,144,128]{2,1,0:T(8,128)(2,1)}), bf16[64,144,128]{2,1,0:T(8,128)(2,1)S(1)}, u32[]{:S(2)}, u32[]{:S(2)}) async-start(bf16[64,144,128]{2,1,0:T(8,128)(2,1)} %reshape_reshape.3), calls=%async_computation.1 | async-start | bytes 4718592 | tf_op jit(solution)/shard_map/all_to_all | solution.py:40
  280.8 4.9 %fusion.22 = bf16[384,1024]{1,0:T(8,128)(2,1)} fusion(bf16[144,8,8,128]{3,2,1,0:T(8,128)(2,1)} %bitcast.50, f32[1152,768]{0,1:T(8,128)} %copy-done.7), kind=kOutput, calls=%fused_computation.34 | convolution fusion | flops 909017088 | bytes 6684672 | tf_op jit(solution)/shard_map/dot_general | solution.py:26
  286.0 5.5 %fusion.17 = bf16[1024,768]{1,0:T(8,128)(2,1)} fusion(bf16[144,8,8,128]{3,2,1,0:T(8,128)(2,1)} %bitcast.49, bf16[1152,384]{0,1:T(8,128)(2,1)} %copy-done.9, bf16[1152,384]{0,1:T(8,128)(2,1)} %copy-done.8), kind=kOutput, calls=%fused_computation.31 | convolution fusion | flops 1816264704 | bytes 5701632 | tf_op jit(solution)/shard_map/dot_general | solution.py:26
  291.6 32.1 %reduce-scatter.5.cloned.1.call-done = bf16[48,1024]{1,0:T(8,128)(2,1)} async-done(((bf16[384,1024]{1,0:T(8,128)(2,1)}), bf16[48,1024]{1,0:T(8,128)(2,1)}) %reduce-scatter.5.cloned.1.call-update) | async-done | bytes 98320 | tf_op jit(solution)/shard_map/reduce_scatter | solution.py:105
  323.6 1.6 bitcast_convert_fusion.1
  325.2 41.5 %reduce-scatter.3.cloned.1.call-done = bf16[128,768]{1,0:T(8,128)(2,1)} async-done(((bf16[1024,768]{1,0:T(8,128)(2,1)}), bf16[128,768]{1,0:T(8,128)(2,1)}) %reduce-scatter.3.cloned.1.call-update) | async-done | bytes 196624 | tf_op jit(solution)/shard_map/reduce_scatter | solution.py:99
  366.7 1.7 bitcast_convert_fusion
  368.4 21.0 %all-to-all-done.1 = bf16[64,144,128]{2,1,0:T(8,128)(2,1)S(1)} async-done(((bf16[64,144,128]{2,1,0:T(8,128)(2,1)}), bf16[64,144,128]{2,1,0:T(8,128)(2,1)S(1)}, u32[]{:S(2)}, u32[]{:S(2)}) %all-to-all-start.1) | async-done | bytes 2359328 | tf_op jit(solution)/shard_map/all_to_all | solution.py:40
  389.5 2.8 copy.16
  392.3 4.2 %fusion.25 = f32[128,1024]{0,1:S(1)} fusion(bf16[1152,1024]{0,1:T(8,128)(2,1)} %bitcast.47, s32[1024]{0:T(1024)S(1)} %get-tuple-element.17, s32[1024]{0:T(1024)S(1)} %get-tuple-element.16), kind=kOutput, calls=%fused_computation.35 | convolution fusion | flops 605437952 | bytes 2891776
  396.5 0.8 copy.17
  (33 shorter events, 1.0 us)
Async XLA Ops:
  7.2 4.2 %copy-start.3 = (bf16[128,1024]{1,0:T(8,128)(2,1)S(1)}, bf16[128,1024]{1,0:T(8,128)(2,1)}, u32[]{:S(2)}) copy-start(bf16[128,1024]{1,0:T(8,128)(2,1)} %param.6) | copy-start | bytes 786436
  7.2 4.3 %copy-start.4 = (bf16[128,1024]{1,0:T(8,128)(2,1)S(1)}, bf16[128,1024]{1,0:T(8,128)(2,1)}, u32[]{:S(2)}) copy-start(bf16[128,1024]{1,0:T(8,128)(2,1)} %param.7) | copy-start | bytes 786436
  16.4 4.6 %copy-start = (bf16[1152,16,128]{2,1,0:T(8,128)(2,1)S(1)}, bf16[1152,16,128]{2,1,0:T(8,128)(2,1)}, u32[]{:S(2)}) copy-start(bf16[1152,16,128]{2,1,0:T(8,128)(2,1)} %gather_fusion) | copy-start | bytes 14155780
  27.9 19.8 %copy-start.5 = (bf16[1,48,1024]{2,1,0:T(8,128)(2,1)S(1)}, bf16[1,48,1024]{2,1,0:T(8,128)(2,1)}, u32[]{:S(2)}) copy-start(bf16[1,48,1024]{2,1,0:T(8,128)(2,1)} %param.11) | copy-start | bytes 294916
  27.9 229.8 %all-to-all-start = ((bf16[64,288,128]{2,1,0:T(8,128)(2,1)}), bf16[64,288,128]{2,1,0:T(8,128)(2,1)}, u32[]{:S(2)}, u32[]{:S(2)}) async-start(bf16[64,288,128]{2,1,0:T(8,128)(2,1)} %bitcast.45), calls=%async_computation | async-start | bytes 9437184 | tf_op jit(solution)/shard_map/all_to_all | solution.py:40
  47.1 214.3 %all-gather.4.cloned.1.call-start = ((), (), s32[]{:S(2)}) async-start(), calls=%async_computation.6 | async-start | bytes 1769472 | tf_op jit(solution)/shard_map/all_gather | solution.py:89
  261.3 4.7 %copy-start.1 = (bf16[1152,8,128]{2,1,0:T(8,128)(2,1)}, bf16[1152,8,128]{2,1,0:T(8,128)(2,1)S(1)}, u32[]{:S(2)}) copy-start(bf16[1152,8,128]{2,1,0:T(8,128)(2,1)S(1)} %get-tuple-element.14) | copy-start | bytes 7077892
  261.3 4.7 %copy-start.2 = (bf16[1152,8,128]{2,1,0:T(8,128)(2,1)S(1)}, bf16[1152,8,128]{2,1,0:T(8,128)(2,1)}, u32[]{:S(2)}) copy-start(bf16[1152,8,128]{2,1,0:T(8,128)(2,1)} %get-tuple-element.15) | copy-start | bytes 7077892
  266.0 1.8 copy-start.7
  266.0 3.0 copy-start.6
  267.8 0.9 copy-start.8
  267.8 1.2 copy-start.9
  273.6 115.9 %all-to-all-start.1 = ((bf16[64,144,128]{2,1,0:T(8,128)(2,1)}), bf16[64,144,128]{2,1,0:T(8,128)(2,1)S(1)}, u32[]{:S(2)}, u32[]{:S(2)}) async-start(bf16[64,144,128]{2,1,0:T(8,128)(2,1)} %reshape_reshape.3), calls=%async_computation.1 | async-start | bytes 4718592 | tf_op jit(solution)/shard_map/all_to_all | solution.py:40
  280.8 42.9 %reduce-scatter.5.cloned.1.call-start = ((), (), s32[]{:S(2)}) async-start(), calls=%async_computation.5 | async-start | bytes 884736 | tf_op jit(solution)/shard_map/reduce_scatter | solution.py:105
  285.7 81.0 %reduce-scatter.3.cloned.1.call-start = ((), (), s32[]{:S(2)}) async-start(), calls=%async_computation.4 | async-start | bytes 1769472 | tf_op jit(solution)/shard_map/reduce_scatter | solution.py:99
Sparse Core Ops, SparseCore 0:
  50.0 31.0 all-gather.3
  285.9 37.7 reduce-scatter.4
  326.5 40.1 reduce-scatter.2
